TPU v7x, 32 devices: a whole 2x2x4 slice. The times are simulated.
32 devices in a mesh: dp: 4 (over y, core), tile: 8 (over z, x).
Axes of the slice: x: 2, y: 2, z: 4, core: 2. Of those that a mesh axis runs over, the one named last changes fastest.
Arguments:
- queries: bfloat16 [4, 8, 1024, 1664], P('dp', 'tile'), may hold values from -48 to 48
- keys: bfloat16 [4, 8, 1024, 1664], P('dp', 'tile'), may hold values from -48 to 48
- values: bfloat16 [4, 8, 1024, 1664], P('dp', 'tile'), may hold values from -6 to 6
- page_info: int32 [4, 5], replicated, may hold values from 0 to 256, as said below
Outputs:
- llm_rows: bfloat16 [9216, 6656], P(('dp', 'tile'))
Inputs may be any that keep to these rules, and one draw needn't show every extreme that they name: `page_info`: columns are 1 to 4, columns times rows is at most 7, tiles fill slots from the first tile slot on within the page, the thumbnail slot lies outside them, text rows at most 256; some page has 7 tiles starting at slot 0, some page 8 - 1 tiles ending at slot 7, and some page 256 text rows.
All inputs are finite; a program needn't handle non-finite values.
Results may differ from a plain program's by a relative error of at most 0.0047.
Values may be sent and summed in bfloat16 or wider, within the bound.
No kernel may reach another device: no remote copies, remote signals or barrier semaphores. Data moves between devices by JAX's collectives and lax.ppermute only.
A program may use at most 256 MiB of HBM per device.

v0:
```python
import jax
import jax.numpy as jnp
from jax import lax
from jax.experimental import pallas as pl
from jax.experimental.pallas import tpu as pltpu
from jax.sharding import PartitionSpec as P

HEADS = 13
HD = 128
GRID = 32
TXTMAX = 256
HH = 1664
TOK = 1024
SHUF = 256
QROWS = 512


def passed_along(value, axis, steps):
    count = lax.axis_size(axis)
    initial, last = (max(0, -steps), min(count, count - steps))
    return lax.ppermute(value, axis, [(source, source + steps) for source in range(initial, last)])


def spread(array, axis, root):
    mine = lax.axis_index(axis) == root
    return lax.psum(jnp.where(mine, array, jnp.zeros_like(array)), axis)


def attention_kernel(flags_ref, q_ref, k0, v0, k1, v1, k2, v2, k3, v3, o_ref, acc_ref, top_ref, sum_ref):
    query = q_ref[...]

    def terms(k_ref, v_ref):
        scores = lax.dot_general(
            query, k_ref[...], (((1,), (1,)), ((), ())), preferred_element_type=jnp.float32
        ) * HD ** (-0.5)
        largest = jnp.max(scores, axis=1, keepdims=True)
        weights = jnp.exp(scores - largest)
        totals = jnp.sum(weights, axis=1, keepdims=True)
        numerator = jnp.dot(weights.astype(jnp.bfloat16), v_ref[...], preferred_element_type=jnp.float32)
        return numerator, largest, totals

    numerator, largest, totals = terms(k0, v0)
    acc_ref[...] = numerator
    top_ref[...] = largest
    sum_ref[...] = totals

    for index, (k_ref, v_ref) in enumerate(((k1, v1), (k2, v2), (k3, v3))):

        @pl.when(flags_ref[index] != 0)
        def _(k_ref=k_ref, v_ref=v_ref):
            numerator, largest, totals = terms(k_ref, v_ref)
            old_top = top_ref[...]
            new_top = jnp.maximum(old_top, largest)
            keep = jnp.exp(old_top - new_top)
            take = jnp.exp(largest - new_top)
            acc_ref[...] = acc_ref[...] * keep + numerator * take
            sum_ref[...] = sum_ref[...] * keep + totals * take
            top_ref[...] = new_top

    o_ref[...] = (acc_ref[...] / sum_ref[...]).astype(o_ref.dtype)


def attend(flags, query_tile, blocks):
    row_spec = pl.BlockSpec((QROWS, HD), lambda h, i, flags: (i, h))
    col_spec = pl.BlockSpec((TOK, HD), lambda h, i, flags: (0, h))
    operands = []
    for key_tile, value_tile in blocks:
        operands += [key_tile, value_tile]
    return pl.pallas_call(
        attention_kernel,
        grid_spec=pltpu.PrefetchScalarGridSpec(
            num_scalar_prefetch=1,
            grid=(HEADS, TOK // QROWS),
            in_specs=[row_spec] + [col_spec] * len(operands),
            out_specs=row_spec,
            scratch_shapes=[
                pltpu.VMEM((QROWS, HD), jnp.float32),
                pltpu.VMEM((QROWS, 1), jnp.float32),
                pltpu.VMEM((QROWS, 1), jnp.float32),
            ],
        ),
        out_shape=jax.ShapeDtypeStruct((TOK, HH), jnp.bfloat16),
    )(flags, query_tile, *operands)


def pixel_shuffle(attended):
    half_grid = GRID // 2
    return (
        attended.reshape(half_grid, 2, half_grid, 2, HH)
        .transpose(0, 2, 1, 3, 4)
        .reshape(half_grid * half_grid, 4 * HH)
    )


def page_layout(page_info):
    columns = page_info[:, 0]
    tile_totals = columns * page_info[:, 1]
    thumbs = page_info[:, 2]
    texts = page_info[:, 3]
    firsts = page_info[:, 4]
    lengths = texts + (tile_totals + 1) * SHUF
    starts = jnp.cumsum(lengths) - lengths
    return (columns, tile_totals, thumbs, texts, starts, firsts)


def body(queries, keys, values, page_info):
    query_tile = queries.reshape(TOK, HH)
    key_tile = keys.reshape(TOK, HH)
    value_tile = values.reshape(TOK, HH)
    slot_count = lax.axis_size("tile")
    page_count = lax.axis_size("dp")
    device_count = page_count * slot_count
    page_index = lax.axis_index("dp")
    slot_index = lax.axis_index("tile")
    columns, tile_totals, thumbs, texts, starts, firsts = page_layout(page_info)
    grid_width = columns[page_index]
    tile_total = tile_totals[page_index]
    thumb_slot = thumbs[page_index]
    grid_pos = slot_index - firsts[page_index]
    is_tile = (grid_pos >= 0) & (grid_pos < tile_total)
    has_left = is_tile & (grid_pos % grid_width > 0)
    has_right = is_tile & (grid_pos % grid_width < grid_width - 1)
    left_keys, left_values = passed_along((key_tile, value_tile), "tile", 1)
    right_keys, right_values = passed_along((key_tile, value_tile), "tile", -1)
    thumb_keys, thumb_values = (
        spread(key_tile, "tile", thumb_slot),
        spread(value_tile, "tile", thumb_slot),
    )
    flags = jnp.stack([has_left, has_right, is_tile]).astype(jnp.int32)
    attended = attend(
        flags,
        query_tile,
        (
            (key_tile, value_tile),
            (left_keys, left_values),
            (right_keys, right_values),
            (thumb_keys, thumb_values),
        ),
    )
    shuffled = pixel_shuffle(attended)
    is_thumb = slot_index == thumb_slot
    is_live = is_tile | is_thumb
    row_start = (
        starts[page_index] + texts[page_index] + jnp.where(is_thumb, tile_total, grid_pos) * SHUF
    )
    per_peer = SHUF // device_count
    arranged = jnp.roll(
        shuffled.reshape(per_peer, device_count, 4 * HH), row_start % device_count, axis=1
    )
    arranged = jnp.where(is_live, arranged, jnp.zeros_like(arranged))
    arrived = lax.all_to_all(arranged, ("dp", "tile"), split_axis=1, concat_axis=1, tiled=True)
    own_rank = page_index * slot_count + slot_index
    sources = jnp.arange(device_count, dtype=jnp.int32)
    source_page = sources // slot_count
    source_slot = sources % slot_count
    source_grid = source_slot - firsts[source_page]
    source_thumb = source_slot == thumbs[source_page]
    source_live = (source_grid >= 0) & (source_grid < tile_totals[source_page]) | source_thumb
    source_start = (
        starts[source_page]
        + texts[source_page]
        + jnp.where(source_thumb, tile_totals[source_page], source_grid) * SHUF
    )
    first_row = (source_start + (own_rank - source_start) % device_count) // device_count
    shard_rows = SHUF + TXTMAX // slot_count
    targets = first_row[None, :] + jnp.arange(per_peer, dtype=jnp.int32)[:, None]
    targets = jnp.where(source_live[None, :], targets, shard_rows)
    placed = jnp.zeros((shard_rows, 4 * HH), jnp.bfloat16)
    return placed.at[targets.reshape(-1)].set(arrived.reshape(-1, 4 * HH), mode="drop")


def solution(mesh):
    placed = (
        P("dp", "tile", None, None),
        P("dp", "tile", None, None),
        P("dp", "tile", None, None),
        P(),
    )
    return jax.shard_map(
        body, mesh=mesh, in_specs=placed, out_specs=P(("dp", "tile"), None), check_vma=False
    )
```

profile of v0, /device:TPU:0, one launch (start us, length us, event | category | flops | bytes accessed | tf_op | source)
XLA Modules:
  0.0 736.2 jit_solution(2041701682982523021)
XLA Ops:
  6.5 0.9 multiply_add_fusion
  8.7 4.1 broadcast_select_fusion
  12.8 2.0 broadcast_select_fusion.1
  14.9 1.3 collective-permute-start.2
  16.2 7.3 collective-permute-start
  23.5 1.3 collective-permute-start.3
  24.7 6.4 collective-permute-start.1
  35.5 1.2 fusion.8
  38.6 68.2 %collective-permute-done.2.k2 = bf16[1024,1664]{1,0:T(8,128)(2,1)} collective-permute-done((bf16[1024,1664]{1,0:T(8,128)(2,1)S(1)}, bf16[1024,1664]{1,0:T(8,128)(2,1)}, u32[]{:S(2)}, u32[]{:S(2)}) %collective-permute-start.2) | collective-permute-done | bytes 3407904 | tf_op jit(solution)/shard_map/ppermute | solution.py:21
  106.8 164.7 %collective-permute-done.k1 = bf16[1024,1664]{1,0:T(8,128)(2,1)} collective-permute-done((bf16[1024,1664]{1,0:T(8,128)(2,1)S(1)}, bf16[1024,1664]{1,0:T(8,128)(2,1)}, u32[]{:S(2)}, u32[]{:S(2)}) %collective-permute-start) | collective-permute-done | bytes 3407904 | tf_op jit(solution)/shard_map/ppermute | solution.py:21
  271.4 102.6 %collective-permute-done.1.v1 = bf16[1024,1664]{1,0:T(8,128)(2,1)} collective-permute-done((bf16[1024,1664]{1,0:T(8,128)(2,1)}, bf16[1024,1664]{1,0:T(8,128)(2,1)}, u32[]{:S(2)}, u32[]{:S(2)}) %collective-permute-start.1) | collective-permute-done | bytes 3407904 | tf_op jit(solution)/shard_map/ppermute | solution.py:21
  374.0 52.6 %all-reduce.3.cloned.1.call-done = (bf16[1024,1664]{1,0:T(8,128)(2,1)}, bf16[1024,1664]{1,0:T(8,128)(2,1)}) async-done(((bf16[1024,1664]{1,0:T(8,128)(2,1)}, bf16[1024,1664]{1,0:T(8,128)(2,1)}), (bf16[1024,1664]{1,0:T(8,128)(2,1)}, bf16[1024,1664]{1,0:T(8,128)(2,1)})) %all-reduce.3.cloned.1.call-update) | async-done | bytes 6815760 | tf_op jit(solution)/shard_map/psum | solution.py:26
  426.6 48.9 %shard_map.46 = bf16[1024,1664]{1,0:T(8,128)(2,1)} custom-call(s32[3]{0:T(128)} %add_convert_fusion.flags_ref, bf16[1024,1664]{1,0:T(8,128)(2,1)} %bitcast.65, bf16[1024,1664]{1,0:T(8,128)(2,1)} %bitcast.58, bf16[1024,1664]{1,0:T(8,128)(2,1)} %bitcast.63, bf16[1024,1664]{1,0:T(8,128)(2,1)} %collective-permute-done.k1, ...), custom_call_target="tpu_custom_call" | custom-call | tf_op jit(solution)/shard_map/pallas_call | solution.py:69
  475.5 6.6 reshape.201
  482.1 4.3 copy.12
  486.5 7.5 %reshape_reshape.3 = bf16[8,32,6656]{2,1,0:T(8,128)(2,1)S(1)} reshape(bf16[16,16,2,2,1664]{4,3,2,1,0:T(2,128)(2,1)} %bitcast.64) | data formatting | bytes 6815744 | tf_op jit(solution)/shard_map/reshape;reshape | solution.py:148
  493.9 2.4 fusion.1
  496.4 3.6 copy.9
  500.0 139.6 %all-to-all-start = ((bf16[8,32,6656]{2,0,1:T(8,128)(2,1)}), bf16[8,32,6656]{2,0,1:T(8,128)(2,1)S(1)}, u32[]{:S(2)}, u32[]{:S(2)}) async-start(bf16[8,32,6656]{2,0,1:T(8,128)(2,1)} %copy.9), calls=%async_computation | async-start | bytes 6815744 | tf_op jit(solution)/shard_map/all_to_all | solution.py:151
  640.3 7.6 %and_or_fusion = (pred[32]{0:T(512)(128)(4,1)S(1)}, s32[32,1]{0,1:T(1,128)S(1)}, s32[32]{0:T(128)S(1)}, pred[32]{0:T(512)(128)(4,1)S(1)}) fusion(s32[]{:T(128)} %bitcast.8, s32[]{:T(128)} %bitcast.7, s32[]{:T(128)} %bitcast.6, s32[]{:T(128)} %bitcast.5, s32[]{:T(128)} %bitcast.3, s32[]{:T(128)} %bitcast.2, s32[]{:T(128)} %bitcast.1, s32[]{:T(128)} %bitcast, ...), kind=kLoop, calls=%fused_computation.26 | loop fusion | flops 1120 | bytes 368 | tf_op jit(solution)/shard_map/or | solution.py:158
  647.9 4.8 and_select_fusion
  652.8 65.1 %all-to-all-done = bf16[8,32,6656]{2,0,1:T(8,128)(2,1)S(1)} async-done(((bf16[8,32,6656]{2,0,1:T(8,128)(2,1)}), bf16[8,32,6656]{2,0,1:T(8,128)(2,1)S(1)}, u32[]{:S(2)}, u32[]{:S(2)}) %all-to-all-start) | async-done | bytes 3407904 | tf_op jit(solution)/shard_map/all_to_all | solution.py:151
  717.9 2.7 copy.10
  720.6 8.8 %scatter_custom_fusion = bf16[288,6656]{1,0:T(8,128)(2,1)} fusion(s32[256]{0:T(256)S(1)} %bitcast.67, bf16[256,6656]{1,0:T(8,128)(2,1)} %bitcast.66, bf16[]{:T(256)} %constant.97.clone.1), kind=kCustom, calls=%fused_computation.8 | custom fusion | bytes 3834368 | tf_op jit(solution)/shard_map/scatter | solution.py:169
  (17 shorter events, 3.2 us)
Async XLA Ops:
  6.5 420.1 %all-reduce.3.cloned.1.call-start = ((), (), s32[]{:S(2)}) async-start(), calls=%async_computation.1 | async-start | bytes 13631488 | tf_op jit(solution)/shard_map/psum | solution.py:26
  8.7 4.2 copy-start
  14.9 91.9 %collective-permute-start.2 = (bf16[1024,1664]{1,0:T(8,128)(2,1)S(1)}, bf16[1024,1664]{1,0:T(8,128)(2,1)}, u32[]{:S(2)}, u32[]{:S(2)}) collective-permute-start(bf16[1024,1664]{1,0:T(8,128)(2,1)S(1)} %bitcast.59), channel_id=1, source_target_pairs={{1,0},{2,1},{3,2},{4,3},{5,4},{6,5},{7,6},{9,8},{10,9},{11,10},{12... | collective-permute-start | bytes 10223624 | tf_op jit(solution)/shard_map/ppermute | solution.py:21
  16.2 255.2 %collective-permute-start = (bf16[1024,1664]{1,0:T(8,128)(2,1)S(1)}, bf16[1024,1664]{1,0:T(8,128)(2,1)}, u32[]{:S(2)}, u32[]{:S(2)}) collective-permute-start(bf16[1024,1664]{1,0:T(8,128)(2,1)S(1)} %bitcast.60), channel_id=1, source_target_pairs={{0,1},{1,2},{2,3},{3,4},{4,5},{5,6},{6,7},{8,9},{9,10},{10,11},{11... | collective-permute-start | bytes 10223624 | tf_op jit(solution)/shard_map/ppermute | solution.py:21
  23.5 248.0 %collective-permute-start.3 = (bf16[1024,1664]{1,0:T(8,128)(2,1)}, bf16[1024,1664]{1,0:T(8,128)(2,1)}, u32[]{:S(2)}, u32[]{:S(2)}) collective-permute-start(bf16[1024,1664]{1,0:T(8,128)(2,1)} %bitcast.61), channel_id=1, source_target_pairs={{1,0},{2,1},{3,2},{4,3},{5,4},{6,5},{7,6},{9,8},{10,9},{11,10},{12... | collective-permute-start | bytes 10223624 | tf_op jit(solution)/shard_map/ppermute | solution.py:21
  24.7 349.3 %collective-permute-start.1 = (bf16[1024,1664]{1,0:T(8,128)(2,1)}, bf16[1024,1664]{1,0:T(8,128)(2,1)}, u32[]{:S(2)}, u32[]{:S(2)}) collective-permute-start(bf16[1024,1664]{1,0:T(8,128)(2,1)} %bitcast.62), channel_id=1, source_target_pairs={{0,1},{1,2},{2,3},{3,4},{4,5},{5,6},{6,7},{8,9},{9,10},{10,11},{11... | collective-permute-start | bytes 10223624 | tf_op jit(solution)/shard_map/ppermute | solution.py:21
  500.0 139.6 %copy-start.1 = (s32[4,5]{1,0:T(4,128)S(1)}, s32[4,5]{1,0:T(4,128)}, u32[]{:S(2)}) copy-start(s32[4,5]{1,0:T(4,128)} %param.7) | copy-start | bytes 244
  500.0 217.9 %all-to-all-start = ((bf16[8,32,6656]{2,0,1:T(8,128)(2,1)}), bf16[8,32,6656]{2,0,1:T(8,128)(2,1)S(1)}, u32[]{:S(2)}, u32[]{:S(2)}) async-start(bf16[8,32,6656]{2,0,1:T(8,128)(2,1)} %copy.9), calls=%async_computation | async-start | bytes 6815744 | tf_op jit(solution)/shard_map/all_to_all | solution.py:151
Sparse Core Ops, SparseCore 0:
  15.0 411.5 all-reduce.2
where the time goes:
time: 737 us; the launch traced here: 736 us
  waiting for transfers between devices  453 us (61%)
  starting transfers between devices  156 us (21%)
  Pallas kernels  48.9 us (7%)
  local copies, waits for them, and re-layouts  36 us (5%)
  other arithmetic  23.8 us (3%)
  between operations  18.5 us (3%)
    ppermute x4, waiting for transfers between devices, passed_along(): lax.ppermute(value, axis, [(source, source + steps) for source in range(i...  335 us
    all_to_all x1, starting transfers between devices, body(): lax.all_to_all(arranged, ('dp', 'tile'), split_axis=1, concat_axis=1, til...  140 us
    all_to_all x1, waiting for transfers between devices, body(): lax.all_to_all(arranged, ('dp', 'tile'), split_axis=1, concat_axis=1, til...  65.1 us
    psum x1, waiting for transfers between devices, spread(): return lax.psum(jnp.where(mine, array, jnp.zeros_like(array)), axis)  52.6 us
    pallas_call x1, Pallas kernels, attend(): pl.pallas_call(attention_kernel, grid_spec=pltpu.PrefetchScalarGridSpec(n...  48.9 us
    ppermute x4, starting transfers between devices, passed_along(): lax.ppermute(value, axis, [(source, source + steps) for source in range(i...  16.2 us
  transfers between devices with their start and end apart: 6, of which 5 were waited for; matrix products, arithmetic and copies ran while one was open for 2% of the time, Pallas kernels for 0%

commit v1 on v0

--- a/solution.py
+++ b/solution.py
@@ -12,7 +12,7 @@
 HH = 1664
 TOK = 1024
 SHUF = 256
-QROWS = 512
+HEAD_CHUNKS = ((0, 4), (4, 8), (8, 13))
 
 
 def passed_along(value, axis, steps):
@@ -21,23 +21,20 @@
     return lax.ppermute(value, axis, [(source, source + steps) for source in range(initial, last)])
 
 
-def spread(array, axis, root):
-    mine = lax.axis_index(axis) == root
-    return lax.psum(jnp.where(mine, array, jnp.zeros_like(array)), axis)
-
-
 def attention_kernel(flags_ref, q_ref, k0, v0, k1, v1, k2, v2, k3, v3, o_ref, acc_ref, top_ref, sum_ref):
     query = q_ref[...]
+    ones = jnp.ones((TOK, HD), jnp.bfloat16)
 
     def terms(k_ref, v_ref):
         scores = lax.dot_general(
             query, k_ref[...], (((1,), (1,)), ((), ())), preferred_element_type=jnp.float32
         ) * HD ** (-0.5)
         largest = jnp.max(scores, axis=1, keepdims=True)
-        weights = jnp.exp(scores - largest)
-        totals = jnp.sum(weights, axis=1, keepdims=True)
-        numerator = jnp.dot(weights.astype(jnp.bfloat16), v_ref[...], preferred_element_type=jnp.float32)
-        return numerator, largest, totals
+        weights = jnp.exp(scores - largest).astype(jnp.bfloat16)
+        both = jnp.dot(
+            weights, jnp.concatenate([v_ref[...], ones], axis=1), preferred_element_type=jnp.float32
+        )
+        return both[:, :HD], largest, both[:, HD : HD + 1]
 
     numerator, largest, totals = terms(k0, v0)
     acc_ref[...] = numerator
@@ -60,35 +57,37 @@
     o_ref[...] = (acc_ref[...] / sum_ref[...]).astype(o_ref.dtype)
 
 
-def attend(flags, query_tile, blocks):
-    row_spec = pl.BlockSpec((QROWS, HD), lambda h, i, flags: (i, h))
-    col_spec = pl.BlockSpec((TOK, HD), lambda h, i, flags: (0, h))
+def attend(flags, query_cols, blocks, head_count):
+    q_spec = pl.BlockSpec((TOK, HD), lambda h, flags: (0, h))
+    k_spec = pl.BlockSpec((TOK, HD), lambda h, flags: (0, h))
+    v_spec = pl.BlockSpec((TOK, HD), lambda h, flags: (0, head_count + h))
     operands = []
-    for key_tile, value_tile in blocks:
-        operands += [key_tile, value_tile]
+    for both in blocks:
+        operands += [both, both]
     return pl.pallas_call(
         attention_kernel,
         grid_spec=pltpu.PrefetchScalarGridSpec(
             num_scalar_prefetch=1,
-            grid=(HEADS, TOK // QROWS),
-            in_specs=[row_spec] + [col_spec] * len(operands),
-            out_specs=row_spec,
+            grid=(head_count,),
+            in_specs=[q_spec] + [k_spec, v_spec] * len(blocks),
+            out_specs=q_spec,
             scratch_shapes=[
-                pltpu.VMEM((QROWS, HD), jnp.float32),
-                pltpu.VMEM((QROWS, 1), jnp.float32),
-                pltpu.VMEM((QROWS, 1), jnp.float32),
+                pltpu.VMEM((TOK, HD), jnp.float32),
+                pltpu.VMEM((TOK, 1), jnp.float32),
+                pltpu.VMEM((TOK, 1), jnp.float32),
             ],
         ),
-        out_shape=jax.ShapeDtypeStruct((TOK, HH), jnp.bfloat16),
-    )(flags, query_tile, *operands)
+        out_shape=jax.ShapeDtypeStruct((TOK, head_count * HD), jnp.bfloat16),
+    )(flags, query_cols, *operands)
 
 
 def pixel_shuffle(attended):
     half_grid = GRID // 2
+    width = attended.shape[-1]
     return (
-        attended.reshape(half_grid, 2, half_grid, 2, HH)
+        attended.reshape(half_grid, 2, half_grid, 2, width)
         .transpose(0, 2, 1, 3, 4)
-        .reshape(half_grid * half_grid, 4 * HH)
+        .reshape(half_grid * half_grid, 4 * width)
     )
 
 
@@ -120,35 +119,39 @@
     is_tile = (grid_pos >= 0) & (grid_pos < tile_total)
     has_left = is_tile & (grid_pos % grid_width > 0)
     has_right = is_tile & (grid_pos % grid_width < grid_width - 1)
-    left_keys, left_values = passed_along((key_tile, value_tile), "tile", 1)
-    right_keys, right_values = passed_along((key_tile, value_tile), "tile", -1)
-    thumb_keys, thumb_values = (
-        spread(key_tile, "tile", thumb_slot),
-        spread(value_tile, "tile", thumb_slot),
-    )
     flags = jnp.stack([has_left, has_right, is_tile]).astype(jnp.int32)
-    attended = attend(
-        flags,
-        query_tile,
-        (
-            (key_tile, value_tile),
-            (left_keys, left_values),
-            (right_keys, right_values),
-            (thumb_keys, thumb_values),
-        ),
-    )
-    shuffled = pixel_shuffle(attended)
     is_thumb = slot_index == thumb_slot
     is_live = is_tile | is_thumb
     row_start = (
         starts[page_index] + texts[page_index] + jnp.where(is_thumb, tile_total, grid_pos) * SHUF
     )
     per_peer = SHUF // device_count
-    arranged = jnp.roll(
-        shuffled.reshape(per_peer, device_count, 4 * HH), row_start % device_count, axis=1
-    )
-    arranged = jnp.where(is_live, arranged, jnp.zeros_like(arranged))
-    arrived = lax.all_to_all(arranged, ("dp", "tile"), split_axis=1, concat_axis=1, tiled=True)
+
+    arrived_parts = []
+    previous_thumb = None
+    for first_head, end_head in HEAD_CHUNKS:
+        head_count = end_head - first_head
+        cols = slice(first_head * HD, end_head * HD)
+        own = jnp.concatenate([key_tile[:, cols], value_tile[:, cols]], axis=1)
+        left = passed_along(own, "tile", 1)
+        right = passed_along(own, "tile", -1)
+        mine = jnp.where(slot_index == thumb_slot, own, jnp.zeros_like(own))
+        if previous_thumb is not None:
+            previous_thumb, mine = lax.optimization_barrier((previous_thumb, mine))
+        thumb = lax.psum(mine, "tile")
+        previous_thumb = thumb
+        attended = attend(flags, query_tile[:, cols], (own, left, right, thumb), head_count)
+        shuffled = pixel_shuffle(attended)
+        arranged = jnp.roll(
+            shuffled.reshape(per_peer, device_count, 4 * head_count * HD),
+            row_start % device_count,
+            axis=1,
+        )
+        arranged = jnp.where(is_live, arranged, jnp.zeros_like(arranged))
+        arrived = lax.all_to_all(arranged, ("dp", "tile"), split_axis=1, concat_axis=1, tiled=True)
+        arrived_parts.append(arrived.reshape(per_peer, device_count, 4, head_count * HD))
+    arrived = jnp.concatenate(arrived_parts, axis=3).reshape(per_peer, device_count, 4 * HH)
+
     own_rank = page_index * slot_count + slot_index
     sources = jnp.arange(device_count, dtype=jnp.int32)
     source_page = sources // slot_count

time: 737 us -> 654 us (0.89); the launches traced: 736 us -> 644 us
  waiting for transfers between devices: 453 us -> 382 us
  starting transfers between devices: 156 us -> 125 us
  local copies, waits for them, and re-layouts: 36 us -> 44.8 us
    ppermute x4 -> x6, waiting for transfers between devices: 335 us -> 0.02 us  [passed_along(): lax.ppermute(value, axis, [(source, source + steps) for source in range(i...]
    psum x1 -> x3, waiting for transfers between devices: 52.6 us -> 363 us  [body(): thumb = lax.psum(mine, 'tile')]
    all_to_all x1 -> x3, waiting for transfers between devices: 65.1 us -> 19.9 us  [body(): lax.all_to_all(arranged, ('dp', 'tile'), split_axis=1, concat_axis=1, til...]
    all_to_all x1 -> x3, starting transfers between devices: 140 us -> 105 us  [body(): lax.all_to_all(arranged, ('dp', 'tile'), split_axis=1, concat_axis=1, til...]
    slice x0 -> x5, local copies, waits for them, and re-layouts: none -> 11.8 us  [the longest x3 6.32 us: body(): own = jnp.concatenate([key_tile[:, cols], value_tile[:, cols]], axis=1)]
    concatenate x0 -> x3, other arithmetic: none -> 8.24 us  [the longest x2 6.56 us: body(): own = jnp.concatenate([key_tile[:, cols], value_tile[:, cols]], axis=1)]
    pallas_call x1 -> x3, Pallas kernels: 48.9 us -> 43.9 us  [attend(): pl.pallas_call(attention_kernel, grid_spec=pltpu.PrefetchScalarGridSpec(n...]
    ppermute x4 -> x6, starting transfers between devices: 16.2 us -> 19.9 us  [passed_along(): lax.ppermute(value, axis, [(source, source + steps) for source in range(i...]
  transfers between devices with their start and end apart: 6 -> 12, of which waited for: 5 -> 4; matrix products, arithmetic and copies ran while one was open for 2% -> 9% of each run, Pallas kernels for 0% -> 7%
where the time goes in v1:
time: 654 us; the launch traced here: 644 us
  waiting for transfers between devices  382 us (58%)
  starting transfers between devices  125 us (19%)
  local copies, waits for them, and re-layouts  44.8 us (7%)
  Pallas kernels  43.9 us (7%)
  other arithmetic  29.5 us (5%)
  between operations  18.8 us (3%)
    psum x3, waiting for transfers between devices, body(): thumb = lax.psum(mine, 'tile')  363 us
    all_to_all x3, starting transfers between devices, body(): lax.all_to_all(arranged, ('dp', 'tile'), split_axis=1, concat_axis=1, til...  105 us
    pallas_call x3, Pallas kernels, attend(): pl.pallas_call(attention_kernel, grid_spec=pltpu.PrefetchScalarGridSpec(n...  43.9 us
    ppermute x6, starting transfers between devices, passed_along(): lax.ppermute(value, axis, [(source, source + steps) for source in range(i...  19.9 us
    all_to_all x3, waiting for transfers between devices, body(): lax.all_to_all(arranged, ('dp', 'tile'), split_axis=1, concat_axis=1, til...  19.9 us
  transfers between devices with their start and end apart: 12, of which 4 were waited for; matrix products, arithmetic and copies ran while one was open for 9% of the time, Pallas kernels for 7%

profile of v1, /device:TPU:0, one launch (start us, length us, event | category | flops | bytes accessed | tf_op | source)
XLA Modules:
  0.0 644.3 jit_solution(2335869763021919179)
XLA Ops:
  8.6 3.5 fusion.12
  14.3 6.2 collective-permute-start
  21.8 4.4 pad_maximum_fusion.3
  26.2 145.5 %all-reduce.4.cloned.1.call-done.k3.v3 = bf16[1024,1024]{1,0:T(8,128)(2,1)} async-done(((bf16[1024,1024]{1,0:T(8,128)(2,1)}), bf16[1024,1024]{1,0:T(8,128)(2,1)}) %all-reduce.4.cloned.1.call-update) | async-done | bytes 2097168 | tf_op jit(solution)/shard_map/psum | solution.py:141
  171.7 4.7 collective-permute-start.2
  184.5 3.0 fusion.11
  188.1 13.8 %shard_map.46 = bf16[1024,512]{1,0:T(8,128)(2,1)} custom-call(s32[3]{0:T(128)} %add_convert_fusion.flags_ref, bf16[1024,512]{1,0:T(8,128)(2,1)} %get-tuple-element.16.q_ref, bf16[1024,1024]{1,0:T(8,128)(2,1)} %copy-done.1, bf16[1024,1024]{1,0:T(8,128)(2,1)} %copy-done.1, bf16[1024,1024]{1,0:T(8,128)(2,1)} %collective-permute-done.k1.v1, ...), custom_call_target="tpu_custom_call" | custom-call | tf_op jit(solution)/shard_map/pallas_call | solution.py:67
  207.7 32.6 %all-to-all-start = ((bf16[8,32,2048]{2,0,1:T(8,128)(2,1)}), bf16[8,32,2048]{2,0,1:T(8,128)(2,1)}, u32[]{:S(2)}, u32[]{:S(2)}) async-start(bf16[8,32,2048]{2,0,1:T(8,128)(2,1)} %copy.9), calls=%async_computation | async-start | bytes 2097152 | tf_op jit(solution)/shard_map/all_to_all | solution.py:151
  243.3 2.3 broadcast_select_fusion
  245.5 5.2 collective-permute-start.4
  252.0 152.8 %all-reduce.6.cloned.1.call-done.k3.v3 = bf16[1024,1024]{1,0:T(8,128)(2,1)} async-done(((bf16[1024,1024]{1,0:T(8,128)(2,1)}), bf16[1024,1024]{1,0:T(8,128)(2,1)}) %all-reduce.6.cloned.1.call-update) | async-done | bytes 2097168 | tf_op jit(solution)/shard_map/psum | solution.py:141
  404.8 13.7 %shard_map.47 = bf16[1024,512]{1,0:T(8,128)(2,1)} custom-call(s32[3]{0:T(128)} %add_convert_fusion.flags_ref, bf16[1024,512]{1,0:T(8,128)(2,1)} %get-tuple-element.17.q_ref, bf16[1024,1024]{1,0:T(8,128)(2,1)} %get-tuple-element.26.k0.v0, bf16[1024,1024]{1,0:T(8,128)(2,1)} %get-tuple-element.26.k0.v0, bf16[1024,1024]{1,0:T(8,128)(2,1)} %collective-permute-done.2.k1.v1, ...), custom_call_target="tpu_custom_call" | custom-call | tf_op jit(solution)/shard_map/pallas_call | solution.py:67
  420.8 3.0 copy.20
  423.8 2.6 reshape_reshape.13
  430.0 32.4 %all-to-all-start.1 = ((bf16[8,32,2048]{2,0,1:T(8,128)(2,1)}), bf16[8,32,2048]{2,0,1:T(8,128)(2,1)}, u32[]{:S(2)}, u32[]{:S(2)}) async-start(bf16[8,32,2048]{2,0,1:T(8,128)(2,1)} %copy.11), calls=%async_computation.1 | async-start | bytes 2097152 | tf_op jit(solution)/shard_map/all_to_all | solution.py:151
  462.4 2.5 slice.126.q_ref
  464.9 64.3 %all-reduce.8.cloned.1.call-done.k3.v3 = bf16[1024,1280]{1,0:T(8,128)(2,1)} async-done(((bf16[1024,1280]{1,0:T(8,128)(2,1)}), bf16[1024,1280]{1,0:T(8,128)(2,1)}) %all-reduce.8.cloned.1.call-update) | async-done | bytes 2621456 | tf_op jit(solution)/shard_map/psum | solution.py:141
  529.2 16.4 %shard_map.48 = bf16[1024,640]{1,0:T(8,128)(2,1)} custom-call(s32[3]{0:T(128)} %add_convert_fusion.flags_ref, bf16[1024,640]{1,0:T(8,128)(2,1)} %slice.126.q_ref, bf16[1024,1280]{1,0:T(8,128)(2,1)} %copy-done, bf16[1024,1280]{1,0:T(8,128)(2,1)} %copy-done, bf16[1024,1280]{1,0:T(8,128)(2,1)} %collective-permute-done.4.k1.v1, ...), custom_call_target="tpu_custom_call" | custom-call | tf_op jit(solution)/shard_map/pallas_call | solution.py:67
  545.6 3.1 reshape.217
  553.5 39.8 %all-to-all-start.2 = ((bf16[8,32,2560]{2,0,1:T(8,128)(2,1)}), bf16[8,32,2560]{2,0,1:T(8,128)(2,1)S(1)}, u32[]{:S(2)}, u32[]{:S(2)}) async-start(bf16[8,32,2560]{2,0,1:T(8,128)(2,1)} %copy.13), calls=%async_computation.2 | async-start | bytes 2621440 | tf_op jit(solution)/shard_map/all_to_all | solution.py:151
  594.1 7.5 %and_or_fusion = (pred[32]{0:T(512)(128)(4,1)S(1)}, s32[32,1]{0,1:T(1,128)S(1)}, s32[32]{0:T(128)S(1)}, pred[32]{0:T(512)(128)(4,1)S(1)}) fusion(s32[]{:T(128)} %bitcast.8, s32[]{:T(128)} %bitcast.7, s32[]{:T(128)} %bitcast.6, s32[]{:T(128)} %bitcast.5, s32[]{:T(128)} %bitcast.3, s32[]{:T(128)} %bitcast.2, s32[]{:T(128)} %bitcast.1, s32[]{:T(128)} %bitcast, ...), kind=kLoop, calls=%fused_computation.41 | loop fusion | flops 1120 | bytes 368 | tf_op jit(solution)/shard_map/or | solution.py:161
  601.6 5.0 and_select_fusion
  606.7 19.9 %all-to-all-done.2 = bf16[8,32,2560]{2,0,1:T(8,128)(2,1)S(1)} async-done(((bf16[8,32,2560]{2,0,1:T(8,128)(2,1)}), bf16[8,32,2560]{2,0,1:T(8,128)(2,1)S(1)}, u32[]{:S(2)}, u32[]{:S(2)}) %all-to-all-start.2) | async-done | bytes 1310752 | tf_op jit(solution)/shard_map/all_to_all | solution.py:151
  630.0 7.4 %scatter_custom_fusion = bf16[288,6656]{1,0:T(8,128)(2,1)} fusion(s32[256]{0:T(256)S(1)} %bitcast.78, bf16[256,6656]{1,0:T(8,128)(2,1)S(1)} %bitcast.73, bf16[]{:T(256)} %constant.118.clone.1), kind=kCustom, calls=%fused_computation.14 | custom fusion | bytes 3833858 | tf_op jit(solution)/shard_map/scatter | solution.py:172
  (53 shorter events, 34.1 us)
Async XLA Ops:
  6.5 165.2 %all-reduce.4.cloned.1.call-start = ((), (), s32[]{:S(2)}) async-start(), calls=%async_computation.3 | async-start | bytes 4194304 | tf_op jit(solution)/shard_map/psum | solution.py:141
  14.2 12.0 %copy-start.1 = (bf16[1024,1024]{1,0:T(8,128)(2,1)}, bf16[1024,1024]{1,0:T(8,128)(2,1)S(1)}, u32[]{:S(2)}) copy-start(bf16[1024,1024]{1,0:T(8,128)(2,1)S(1)} %get-tuple-element.24.k0.v0) | copy-start | bytes 6291460
  14.3 390.5 %all-reduce.6.cloned.1.call-start = ((), (), s32[]{:S(2)}) async-start(), calls=%async_computation.4 | async-start | bytes 4194304 | tf_op jit(solution)/shard_map/psum | solution.py:141
  14.3 173.8 %collective-permute-start = (bf16[1024,1024]{1,0:T(8,128)(2,1)S(1)}, bf16[1024,1024]{1,0:T(8,128)(2,1)}, u32[]{:S(2)}, u32[]{:S(2)}) collective-permute-start(bf16[1024,1024]{1,0:T(8,128)(2,1)S(1)} %get-tuple-element.24.k0.v0), channel_id=1, source_target_pairs={{0,1},{1,2},{2,3},{3,4},{4,5},{5,6},{6,7},{8,9},{9,10},{10,11},{11... | collective-permute-start | bytes 6291464 | tf_op jit(solution)/shard_map/ppermute | solution.py:21
  20.5 167.6 %collective-permute-start.1 = (bf16[1024,1024]{1,0:T(8,128)(2,1)S(1)}, bf16[1024,1024]{1,0:T(8,128)(2,1)}, u32[]{:S(2)}, u32[]{:S(2)}) collective-permute-start(bf16[1024,1024]{1,0:T(8,128)(2,1)S(1)} %get-tuple-element.24.k0.v0), channel_id=1, source_target_pairs={{1,0},{2,1},{3,2},{4,3},{5,4},{6,5},{7,6},{9,8},{10,9},{11,10},{12... | collective-permute-start | bytes 6291464 | tf_op jit(solution)/shard_map/ppermute | solution.py:21
  171.7 233.1 %collective-permute-start.2 = (bf16[1024,1024]{1,0:T(8,128)(2,1)}, bf16[1024,1024]{1,0:T(8,128)(2,1)}, u32[]{:S(2)}, u32[]{:S(2)}) collective-permute-start(bf16[1024,1024]{1,0:T(8,128)(2,1)} %get-tuple-element.26.k0.v0), channel_id=1, source_target_pairs={{0,1},{1,2},{2,3},{3,4},{4,5},{5,6},{6,7},{8,9},{9,10},{10,11},{11... | collective-permute-start | bytes 6291464 | tf_op jit(solution)/shard_map/ppermute | solution.py:21
  176.4 228.4 %collective-permute-start.3 = (bf16[1024,1024]{1,0:T(8,128)(2,1)}, bf16[1024,1024]{1,0:T(8,128)(2,1)}, u32[]{:S(2)}, u32[]{:S(2)}) collective-permute-start(bf16[1024,1024]{1,0:T(8,128)(2,1)} %get-tuple-element.26.k0.v0), channel_id=1, source_target_pairs={{1,0},{2,1},{3,2},{4,3},{5,4},{6,5},{7,6},{9,8},{10,9},{11,10},{12... | collective-permute-start | bytes 6291464 | tf_op jit(solution)/shard_map/ppermute | solution.py:21
  207.7 222.3 %all-to-all-start = ((bf16[8,32,2048]{2,0,1:T(8,128)(2,1)}), bf16[8,32,2048]{2,0,1:T(8,128)(2,1)}, u32[]{:S(2)}, u32[]{:S(2)}) async-start(bf16[8,32,2048]{2,0,1:T(8,128)(2,1)} %copy.9), calls=%async_computation | async-start | bytes 2097152 | tf_op jit(solution)/shard_map/all_to_all | solution.py:151
  240.3 288.9 %all-reduce.8.cloned.1.call-start = ((), (), s32[]{:S(2)}) async-start(), calls=%async_computation.5 | async-start | bytes 5242880 | tf_op jit(solution)/shard_map/psum | solution.py:141
  245.5 173.0 %copy-start = (bf16[1024,1280]{1,0:T(8,128)(2,1)}, bf16[1024,1280]{1,0:T(8,128)(2,1)S(1)}, u32[]{:S(2)}) copy-start(bf16[1024,1280]{1,0:T(8,128)(2,1)S(1)} %get-tuple-element.23.k0.v0) | copy-start | bytes 7864324
  245.5 219.4 %collective-permute-start.4 = (bf16[1024,1280]{1,0:T(8,128)(2,1)S(1)}, bf16[1024,1280]{1,0:T(8,128)(2,1)}, u32[]{:S(2)}, u32[]{:S(2)}) collective-permute-start(bf16[1024,1280]{1,0:T(8,128)(2,1)S(1)} %get-tuple-element.23.k0.v0), channel_id=1, source_target_pairs={{0,1},{1,2},{2,3},{3,4},{4,5},{5,6},{6,7},{8,9},{9,10},{10,11},{11... | collective-permute-start | bytes 7864328 | tf_op jit(solution)/shard_map/ppermute | solution.py:21
  250.7 214.2 %collective-permute-start.5 = (bf16[1024,1280]{1,0:T(8,128)(2,1)S(1)}, bf16[1024,1280]{1,0:T(8,128)(2,1)}, u32[]{:S(2)}, u32[]{:S(2)}) collective-permute-start(bf16[1024,1280]{1,0:T(8,128)(2,1)S(1)} %get-tuple-element.23.k0.v0), channel_id=1, source_target_pairs={{1,0},{2,1},{3,2},{4,3},{5,4},{6,5},{7,6},{9,8},{10,9},{11,10},{12... | collective-permute-start | bytes 7864328 | tf_op jit(solution)/shard_map/ppermute | solution.py:21
  430.0 123.5 %all-to-all-start.1 = ((bf16[8,32,2048]{2,0,1:T(8,128)(2,1)}), bf16[8,32,2048]{2,0,1:T(8,128)(2,1)}, u32[]{:S(2)}, u32[]{:S(2)}) async-start(bf16[8,32,2048]{2,0,1:T(8,128)(2,1)} %copy.11), calls=%async_computation.1 | async-start | bytes 2097152 | tf_op jit(solution)/shard_map/all_to_all | solution.py:151
  551.7 41.6 %copy-start.2 = (s32[4,5]{1,0:T(4,128)S(1)}, s32[4,5]{1,0:T(4,128)}, u32[]{:S(2)}) copy-start(s32[4,5]{1,0:T(4,128)} %param.9) | copy-start | bytes 244
  553.5 73.0 %all-to-all-start.2 = ((bf16[8,32,2560]{2,0,1:T(8,128)(2,1)}), bf16[8,32,2560]{2,0,1:T(8,128)(2,1)S(1)}, u32[]{:S(2)}, u32[]{:S(2)}) async-start(bf16[8,32,2560]{2,0,1:T(8,128)(2,1)} %copy.13), calls=%async_computation.2 | async-start | bytes 2621440 | tf_op jit(solution)/shard_map/all_to_all | solution.py:151
Sparse Core Ops, SparseCore 0:
  14.4 157.2 all-reduce.3
  175.3 229.4 all-reduce.5
  408.5 120.7 all-reduce.7

commit v2 on v1

--- a/solution.py
+++ b/solution.py
@@ -21,55 +21,83 @@
     return lax.ppermute(value, axis, [(source, source + steps) for source in range(initial, last)])
 
 
-def attention_kernel(flags_ref, q_ref, k0, v0, k1, v1, k2, v2, k3, v3, o_ref, acc_ref, top_ref, sum_ref):
+def block_terms(query, k_ref, v_ref):
+    scores = lax.dot_general(
+        query, k_ref[...], (((1,), (1,)), ((), ())), preferred_element_type=jnp.float32
+    ) * HD ** (-0.5)
+    largest = jnp.max(scores, axis=1, keepdims=True)
+    weights = jnp.exp(scores - largest).astype(jnp.bfloat16)
+    ones = jnp.ones((TOK, HD), jnp.bfloat16)
+    both = jnp.dot(
+        weights, jnp.concatenate([v_ref[...], ones], axis=1), preferred_element_type=jnp.float32
+    )
+    return both[:, :HD], largest, both[:, HD : HD + 1]
+
+
+def merge_block(flag, query, k_ref, v_ref, acc_ref, top_ref, sum_ref):
+    @pl.when(flag != 0)
+    def _():
+        numerator, largest, totals = block_terms(query, k_ref, v_ref)
+        old_top = top_ref[...]
+        new_top = jnp.maximum(old_top, largest)
+        keep = jnp.exp(old_top - new_top)
+        take = jnp.exp(largest - new_top)
+        acc_ref[...] = acc_ref[...] * keep + numerator * take
+        sum_ref[...] = sum_ref[...] * keep + totals * take
+        top_ref[...] = new_top
+
+
+def near_kernel(flags_ref, q_ref, k0, v0, k1, v1, k2, v2, acc_ref, top_ref, sum_ref):
     query = q_ref[...]
-    ones = jnp.ones((TOK, HD), jnp.bfloat16)
-
-    def terms(k_ref, v_ref):
-        scores = lax.dot_general(
-            query, k_ref[...], (((1,), (1,)), ((), ())), preferred_element_type=jnp.float32
-        ) * HD ** (-0.5)
-        largest = jnp.max(scores, axis=1, keepdims=True)
-        weights = jnp.exp(scores - largest).astype(jnp.bfloat16)
-        both = jnp.dot(
-            weights, jnp.concatenate([v_ref[...], ones], axis=1), preferred_element_type=jnp.float32
-        )
-        return both[:, :HD], largest, both[:, HD : HD + 1]
-
-    numerator, largest, totals = terms(k0, v0)
+    numerator, largest, totals = block_terms(query, k0, v0)
     acc_ref[...] = numerator
-    top_ref[...] = largest
-    sum_ref[...] = totals
-
-    for index, (k_ref, v_ref) in enumerate(((k1, v1), (k2, v2), (k3, v3))):
-
-        @pl.when(flags_ref[index] != 0)
-        def _(k_ref=k_ref, v_ref=v_ref):
-            numerator, largest, totals = terms(k_ref, v_ref)
-            old_top = top_ref[...]
-            new_top = jnp.maximum(old_top, largest)
-            keep = jnp.exp(old_top - new_top)
-            take = jnp.exp(largest - new_top)
-            acc_ref[...] = acc_ref[...] * keep + numerator * take
-            sum_ref[...] = sum_ref[...] * keep + totals * take
-            top_ref[...] = new_top
-
+    top_ref[0] = largest
+    sum_ref[0] = totals
+    merge_block(flags_ref[0], query, k1, v1, acc_ref, top_ref.at[0], sum_ref.at[0])
+    merge_block(flags_ref[1], query, k2, v2, acc_ref, top_ref.at[0], sum_ref.at[0])
+
+
+def thumb_kernel(flags_ref, q_ref, k3, v3, acc_in, top_in, sum_in, o_ref, acc_ref, top_ref, sum_ref):
+    acc_ref[...] = acc_in[...]
+    top_ref[...] = top_in[0]
+    sum_ref[...] = sum_in[0]
+    merge_block(flags_ref[2], q_ref[...], k3, v3, acc_ref, top_ref, sum_ref)
     o_ref[...] = (acc_ref[...] / sum_ref[...]).astype(o_ref.dtype)
 
 
-def attend(flags, query_cols, blocks, head_count):
+def attend_near(flags, query_cols, blocks, head_count):
     q_spec = pl.BlockSpec((TOK, HD), lambda h, flags: (0, h))
-    k_spec = pl.BlockSpec((TOK, HD), lambda h, flags: (0, h))
     v_spec = pl.BlockSpec((TOK, HD), lambda h, flags: (0, head_count + h))
+    stat_spec = pl.BlockSpec((1, TOK, 1), lambda h, flags: (h, 0, 0))
     operands = []
     for both in blocks:
         operands += [both, both]
     return pl.pallas_call(
-        attention_kernel,
+        near_kernel,
         grid_spec=pltpu.PrefetchScalarGridSpec(
             num_scalar_prefetch=1,
             grid=(head_count,),
-            in_specs=[q_spec] + [k_spec, v_spec] * len(blocks),
+            in_specs=[q_spec] + [q_spec, v_spec] * len(blocks),
+            out_specs=[q_spec, stat_spec, stat_spec],
+        ),
+        out_shape=[
+            jax.ShapeDtypeStruct((TOK, head_count * HD), jnp.float32),
+            jax.ShapeDtypeStruct((head_count, TOK, 1), jnp.float32),
+            jax.ShapeDtypeStruct((head_count, TOK, 1), jnp.float32),
+        ],
+    )(flags, query_cols, *operands)
+
+
+def attend_thumb(flags, query_tile, thumb, acc, top, totals):
+    q_spec = pl.BlockSpec((TOK, HD), lambda h, flags: (0, h))
+    v_spec = pl.BlockSpec((TOK, HD), lambda h, flags: (0, HEADS + h))
+    stat_spec = pl.BlockSpec((1, TOK, 1), lambda h, flags: (h, 0, 0))
+    return pl.pallas_call(
+        thumb_kernel,
+        grid_spec=pltpu.PrefetchScalarGridSpec(
+            num_scalar_prefetch=1,
+            grid=(HEADS,),
+            in_specs=[q_spec, q_spec, v_spec, q_spec, stat_spec, stat_spec],
             out_specs=q_spec,
             scratch_shapes=[
                 pltpu.VMEM((TOK, HD), jnp.float32),
@@ -77,8 +105,8 @@
                 pltpu.VMEM((TOK, 1), jnp.float32),
             ],
         ),
-        out_shape=jax.ShapeDtypeStruct((TOK, head_count * HD), jnp.bfloat16),
-    )(flags, query_cols, *operands)
+        out_shape=jax.ShapeDtypeStruct((TOK, HH), jnp.bfloat16),
+    )(flags, query_tile, thumb, thumb, acc, top, totals)
 
 
 def pixel_shuffle(attended):
@@ -127,31 +155,28 @@
     )
     per_peer = SHUF // device_count
 
-    arrived_parts = []
-    previous_thumb = None
+    mine = jnp.where(
+        slot_index == thumb_slot,
+        jnp.concatenate([key_tile, value_tile], axis=1),
+        jnp.zeros((TOK, 2 * HH), jnp.bfloat16),
+    )
+    thumb = lax.psum(mine, "tile")
+    states = []
     for first_head, end_head in HEAD_CHUNKS:
         head_count = end_head - first_head
         cols = slice(first_head * HD, end_head * HD)
         own = jnp.concatenate([key_tile[:, cols], value_tile[:, cols]], axis=1)
         left = passed_along(own, "tile", 1)
         right = passed_along(own, "tile", -1)
-        mine = jnp.where(slot_index == thumb_slot, own, jnp.zeros_like(own))
-        if previous_thumb is not None:
-            previous_thumb, mine = lax.optimization_barrier((previous_thumb, mine))
-        thumb = lax.psum(mine, "tile")
-        previous_thumb = thumb
-        attended = attend(flags, query_tile[:, cols], (own, left, right, thumb), head_count)
-        shuffled = pixel_shuffle(attended)
-        arranged = jnp.roll(
-            shuffled.reshape(per_peer, device_count, 4 * head_count * HD),
-            row_start % device_count,
-            axis=1,
-        )
-        arranged = jnp.where(is_live, arranged, jnp.zeros_like(arranged))
-        arrived = lax.all_to_all(arranged, ("dp", "tile"), split_axis=1, concat_axis=1, tiled=True)
-        arrived_parts.append(arrived.reshape(per_peer, device_count, 4, head_count * HD))
-    arrived = jnp.concatenate(arrived_parts, axis=3).reshape(per_peer, device_count, 4 * HH)
-
+        states.append(attend_near(flags, query_tile[:, cols], (own, left, right), head_count))
+    acc, top, totals = (jnp.concatenate(parts, axis=axis) for parts, axis in zip(zip(*states), (1, 0, 0)))
+    attended = attend_thumb(flags, query_tile, thumb, acc, top, totals)
+    shuffled = pixel_shuffle(attended)
+    arranged = jnp.roll(
+        shuffled.reshape(per_peer, device_count, 4 * HH), row_start % device_count, axis=1
+    )
+    arranged = jnp.where(is_live, arranged, jnp.zeros_like(arranged))
+    arrived = lax.all_to_all(arranged, ("dp", "tile"), split_axis=1, concat_axis=1, tiled=True)
     own_rank = page_index * slot_count + slot_index
     sources = jnp.arange(device_count, dtype=jnp.int32)
     source_page = sources // slot_count

time: 654 us -> 648 us (level); the launches traced: 644 us -> 649 us
  waiting for transfers between devices: 382 us -> 329 us
  local copies, waits for them, and re-layouts: 44.8 us -> 68.3 us
  Pallas kernels: 43.9 us -> 59.9 us
  starting transfers between devices: 125 us -> 138 us
    psum x3 -> x1, waiting for transfers between devices: 363 us -> 0.01 us  [body(): thumb = lax.psum(mine, 'tile')]
    ppermute x6, waiting for transfers between devices: 0.02 us -> 265 us  [passed_along(): lax.ppermute(value, axis, [(source, source + steps) for source in range(i...]
    all_to_all x3 -> x1, waiting for transfers between devices: 19.9 us -> 64.7 us  [body(): lax.all_to_all(arranged, ('dp', 'tile'), split_axis=1, concat_axis=1, til...]
    ppermute x6, starting transfers between devices: 19.9 us -> 63.3 us  [passed_along(): lax.ppermute(value, axis, [(source, source + steps) for source in range(i...]
    all_to_all x3 -> x1, starting transfers between devices: 105 us -> 74.6 us  [body(): lax.all_to_all(arranged, ('dp', 'tile'), split_axis=1, concat_axis=1, til...]
    pallas_call x3 -> x4, Pallas kernels: 43.9 us -> 59.9 us  [the longest x3 42.8 us: attend_near(): pl.pallas_call(near_kernel, grid_spec=pltpu.PrefetchScalarGridSpec(num_sc...]
    pallas_call x0 -> x6, local copies, waits for them, and re-layouts: none -> 12.4 us  [attend_near(): pl.pallas_call(near_kernel, grid_spec=pltpu.PrefetchScalarGridSpec(num_sc...]
    concatenate x1 -> x2, local copies, waits for them, and re-layouts: 1.32 us -> 8.69 us  [body(): jnp.concatenate(parts, axis=axis)]
  transfers between devices with their start and end apart: 12 -> 8, of which waited for: 4 -> 4; matrix products, arithmetic and copies ran while one was open for 9% -> 9% of each run, Pallas kernels for 7% -> 7%
where the time goes in v2:
time: 648 us; the launch traced here: 649 us
  waiting for transfers between devices  329 us (51%)
  starting transfers between devices  138 us (21%)
  local copies, waits for them, and re-layouts  68.3 us (11%)
  Pallas kernels  59.9 us (9%)
  other arithmetic  34.1 us (5%)
  between operations  19.2 us (3%)
    ppermute x6, waiting for transfers between devices, passed_along(): lax.ppermute(value, axis, [(source, source + steps) for source in range(i...  265 us
    all_to_all x1, starting transfers between devices, body(): lax.all_to_all(arranged, ('dp', 'tile'), split_axis=1, concat_axis=1, til...  74.6 us
    all_to_all x1, waiting for transfers between devices, body(): lax.all_to_all(arranged, ('dp', 'tile'), split_axis=1, concat_axis=1, til...  64.7 us
    ppermute x6, starting transfers between devices, passed_along(): lax.ppermute(value, axis, [(source, source + steps) for source in range(i...  63.3 us
    pallas_call x3, Pallas kernels, attend_near(): pl.pallas_call(near_kernel, grid_spec=pltpu.PrefetchScalarGridSpec(num_sc...  42.8 us
    pallas_call x1, Pallas kernels, attend_thumb(): pl.pallas_call(thumb_kernel, grid_spec=pltpu.PrefetchScalarGridSpec(num_s...  17.1 us
  transfers between devices with their start and end apart: 8, of which 4 were waited for; matrix products, arithmetic and copies ran while one was open for 9% of the time, Pallas kernels for 7%

profile of v2, /device:TPU:0, one launch (start us, length us, event | category | flops | bytes accessed | tf_op | source)
XLA Modules:
  0.0 648.9 jit_solution(18181537790300104877)
XLA Ops:
  8.7 7.0 %maximum_select_fusion = bf16[1024,3328]{1,0:T(8,128)(2,1)} fusion(bf16[1024,1664]{1,0:T(8,128)(2,1)} %bitcast.60, bf16[1024,1664]{1,0:T(8,128)(2,1)} %bitcast.57, pred[]{:T(512)S(6)} %eq.27), kind=kLoop, calls=%fused_computation.1 | loop fusion | flops 17039360 | bytes 13631489 | tf_op jit(solution)/shard_map/jit(_where)/select_n | solution.py:158
  25.9 7.5 %collective-permute-start.4 = (bf16[1024,1280]{1,0:T(8,128)(2,1)S(1)}, bf16[1024,1280]{1,0:T(8,128)(2,1)}, u32[]{:S(2)}, u32[]{:S(2)}) collective-permute-start(bf16[1024,1280]{1,0:T(8,128)(2,1)S(1)} %pad_maximum_fusion.1.k0.v0), channel_id=1, source_target_pairs={{0,1},{1,2},{2,3},{3,4},{4,5},{5,6},{6,7},{8,9},{9,10},{10,11},{11... | collective-permute-start | bytes 7864328 | tf_op jit(solution)/shard_map/ppermute | solution.py:21
  33.4 4.7 collective-permute-start.2
  41.0 52.6 %collective-permute-done.3.k2.v2 = bf16[1024,1024]{1,0:T(8,128)(2,1)} collective-permute-done((bf16[1024,1024]{1,0:T(8,128)(2,1)}, bf16[1024,1024]{1,0:T(8,128)(2,1)}, u32[]{:S(2)}, u32[]{:S(2)}) %collective-permute-start.3) | collective-permute-done | bytes 2097184 | tf_op jit(solution)/shard_map/ppermute | solution.py:21
  93.7 47.2 %collective-permute-start = (bf16[1024,1024]{1,0:T(8,128)(2,1)}, bf16[1024,1024]{1,0:T(8,128)(2,1)}, u32[]{:S(2)}, u32[]{:S(2)}) collective-permute-start(bf16[1024,1024]{1,0:T(8,128)(2,1)} %pad_maximum_fusion.2.k0.v0), channel_id=1, source_target_pairs={{0,1},{1,2},{2,3},{3,4},{4,5},{5,6},{6,7},{8,9},{9,10},{10,11},{11... | collective-permute-start | bytes 6291464 | tf_op jit(solution)/shard_map/ppermute | solution.py:21
  151.0 3.0 fusion.9
  154.0 166.1 %collective-permute-done.2.k1.v1 = bf16[1024,1024]{1,0:T(8,128)(2,1)} collective-permute-done((bf16[1024,1024]{1,0:T(8,128)(2,1)}, bf16[1024,1024]{1,0:T(8,128)(2,1)}, u32[]{:S(2)}, u32[]{:S(2)}) %collective-permute-start.2) | collective-permute-done | bytes 2097184 | tf_op jit(solution)/shard_map/ppermute | solution.py:21
  320.1 13.2 %shard_map.47 = (f32[1024,512]{1,0:T(8,128)}, f32[4,1024,1]{2,1,0:T(8,128)}, f32[4,1024,1]{2,1,0:T(8,128)}) custom-call(s32[3]{0:T(128)} %add_convert_fusion.flags_ref, bf16[1024,512]{1,0:T(8,128)(2,1)} %get-tuple-element.34.q_ref, bf16[1024,1024]{1,0:T(8,128)(2,1)} %pad_maximum_fusion.3.k0.v0, bf16[1024,1024]{1,0:T(8,128)(2,1)} %pad_maximum_fusion.3.k0.v0, ...), custom_call_target="tpu_custom_call" | custom-call | tf_op jit(solution)/shard_map/pallas_call | solution.py:75
  337.8 46.0 %collective-permute-done.k1.v1 = bf16[1024,1024]{1,0:T(8,128)(2,1)} collective-permute-done((bf16[1024,1024]{1,0:T(8,128)(2,1)}, bf16[1024,1024]{1,0:T(8,128)(2,1)}, u32[]{:S(2)}, u32[]{:S(2)}) %collective-permute-start) | collective-permute-done | bytes 2097184 | tf_op jit(solution)/shard_map/ppermute | solution.py:21
  383.8 13.6 %shard_map.46 = (f32[1024,512]{1,0:T(8,128)}, f32[4,1024,1]{2,1,0:T(8,128)}, f32[4,1024,1]{2,1,0:T(8,128)}) custom-call(s32[3]{0:T(128)} %add_convert_fusion.flags_ref, bf16[1024,512]{1,0:T(8,128)(2,1)} %get-tuple-element.33.q_ref, bf16[1024,1024]{1,0:T(8,128)(2,1)} %pad_maximum_fusion.2.k0.v0, bf16[1024,1024]{1,0:T(8,128)(2,1)} %pad_maximum_fusion.2.k0.v0, ...), custom_call_target="tpu_custom_call" | custom-call | tf_op jit(solution)/shard_map/pallas_call | solution.py:75
  401.9 15.9 %shard_map.48 = (f32[1024,640]{1,0:T(8,128)}, f32[5,1024,1]{2,1,0:T(8,128)}, f32[5,1024,1]{2,1,0:T(8,128)}) custom-call(s32[3]{0:T(128)} %add_convert_fusion.flags_ref, bf16[1024,640]{1,0:T(8,128)(2,1)} %slice.126.q_ref, bf16[1024,1280]{1,0:T(8,128)(2,1)} %copy-done, bf16[1024,1280]{1,0:T(8,128)(2,1)} %copy-done, ...), custom_call_target="tpu_custom_call" | custom-call | tf_op jit(solution)/shard_map/pallas_call | solution.py:75
  421.3 4.3 copy.23.sum_in
  425.7 4.3 copy.22.top_in
  430.0 5.5 pad_maximum_fusion.acc_in
  435.5 17.1 %shard_map.49 = bf16[1024,1664]{1,0:T(8,128)(2,1)} custom-call(s32[3]{0:T(128)} %add_convert_fusion.flags_ref, bf16[1024,1664]{1,0:T(8,128)(2,1)} %bitcast.65, bf16[1024,3328]{1,0:T(8,128)(2,1)} %all-reduce.2.cloned.1.call-done.k3.v3, bf16[1024,3328]{1,0:T(8,128)(2,1)} %all-reduce.2.cloned.1.call-done.k3.v3, f32[1024,1664]{1,0:T(8,128)} %pad_maximum_fusion.acc_in, ...), custom_call_target="tpu_custom_call" | custom-call | tf_op jit(solution)/shard_map/pallas_call | solution.py:95
  452.7 6.6 %reshape.201 = bf16[16,2,16,2,1664]{4,3,2,1,0:T(2,128)(2,1)S(1)} reshape(bf16[1024,1664]{1,0:T(8,128)(2,1)} %shard_map.49) | data formatting | bytes 6815744 | tf_op jit(solution)/shard_map/reshape | solution.py:116
  459.3 4.3 copy.28
  463.6 7.5 %reshape_reshape.3 = bf16[8,32,6656]{2,1,0:T(8,128)(2,1)S(1)} reshape(bf16[16,16,2,2,1664]{4,3,2,1,0:T(2,128)(2,1)} %bitcast.56) | data formatting | bytes 6815744 | tf_op jit(solution)/shard_map/reshape;reshape | solution.py:176
  473.6 3.6 copy.25
  477.2 74.6 %all-to-all-start = ((bf16[8,32,6656]{2,0,1:T(8,128)(2,1)}), bf16[8,32,6656]{2,0,1:T(8,128)(2,1)S(1)}, u32[]{:S(2)}, u32[]{:S(2)}) async-start(bf16[8,32,6656]{2,0,1:T(8,128)(2,1)} %copy.25), calls=%async_computation | async-start | bytes 6815744 | tf_op jit(solution)/shard_map/all_to_all | solution.py:179
  552.5 7.6 %and_or_fusion = (pred[32]{0:T(512)(128)(4,1)S(1)}, s32[32,1]{0,1:T(1,128)S(1)}, s32[32]{0:T(128)S(1)}, pred[32]{0:T(512)(128)(4,1)S(1)}) fusion(s32[]{:T(128)} %bitcast.8, s32[]{:T(128)} %bitcast.7, s32[]{:T(128)} %bitcast.6, s32[]{:T(128)} %bitcast.5, s32[]{:T(128)} %bitcast.3, s32[]{:T(128)} %bitcast.2, s32[]{:T(128)} %bitcast.1, s32[]{:T(128)} %bitcast, ...), kind=kLoop, calls=%fused_computation.31 | loop fusion | flops 1120 | bytes 368 | tf_op jit(solution)/shard_map/or | solution.py:186
  560.1 5.1 and_select_fusion
  565.3 64.7 %all-to-all-done = bf16[8,32,6656]{2,0,1:T(8,128)(2,1)S(1)} async-done(((bf16[8,32,6656]{2,0,1:T(8,128)(2,1)}), bf16[8,32,6656]{2,0,1:T(8,128)(2,1)S(1)}, u32[]{:S(2)}, u32[]{:S(2)}) %all-to-all-start) | async-done | bytes 3407904 | tf_op jit(solution)/shard_map/all_to_all | solution.py:179
  632.8 8.8 %scatter_custom_fusion = bf16[288,6656]{1,0:T(8,128)(2,1)} fusion(s32[256]{0:T(256)S(1)} %bitcast.67, bf16[256,6656]{1,0:T(8,128)(2,1)} %bitcast.66, bf16[]{:T(256)} %constant.97.clone.1), kind=kCustom, calls=%fused_computation.11 | custom fusion | bytes 3834368 | tf_op jit(solution)/shard_map/scatter | solution.py:197
  (48 shorter events, 38.5 us)
Async XLA Ops:
  6.5 429.0 %all-reduce.2.cloned.1.call-start = ((), (), s32[]{:S(2)}) async-start(), calls=%async_computation.1 | async-start | bytes 13631488 | tf_op jit(solution)/shard_map/psum | solution.py:163
  15.8 2.0 copy-start.1
  21.4 72.3 %collective-permute-start.3 = (bf16[1024,1024]{1,0:T(8,128)(2,1)}, bf16[1024,1024]{1,0:T(8,128)(2,1)}, u32[]{:S(2)}, u32[]{:S(2)}) collective-permute-start(bf16[1024,1024]{1,0:T(8,128)(2,1)} %pad_maximum_fusion.3.k0.v0), channel_id=1, source_target_pairs={{1,0},{2,1},{3,2},{4,3},{5,4},{6,5},{7,6},{9,8},{10,9},{11,10},{12... | collective-permute-start | bytes 6291464 | tf_op jit(solution)/shard_map/ppermute | solution.py:21
  24.6 125.7 %copy-start = (bf16[1024,1280]{1,0:T(8,128)(2,1)}, bf16[1024,1280]{1,0:T(8,128)(2,1)S(1)}, u32[]{:S(2)}) copy-start(bf16[1024,1280]{1,0:T(8,128)(2,1)S(1)} %pad_maximum_fusion.1.k0.v0) | copy-start | bytes 7864324
  24.6 377.3 %collective-permute-start.5 = (bf16[1024,1280]{1,0:T(8,128)(2,1)S(1)}, bf16[1024,1280]{1,0:T(8,128)(2,1)}, u32[]{:S(2)}, u32[]{:S(2)}) collective-permute-start(bf16[1024,1280]{1,0:T(8,128)(2,1)S(1)} %pad_maximum_fusion.1.k0.v0), channel_id=1, source_target_pairs={{1,0},{2,1},{3,2},{4,3},{5,4},{6,5},{7,6},{9,8},{10,9},{11,10},{12... | collective-permute-start | bytes 7864328 | tf_op jit(solution)/shard_map/ppermute | solution.py:21
  25.9 376.0 %collective-permute-start.4 = (bf16[1024,1280]{1,0:T(8,128)(2,1)S(1)}, bf16[1024,1280]{1,0:T(8,128)(2,1)}, u32[]{:S(2)}, u32[]{:S(2)}) collective-permute-start(bf16[1024,1280]{1,0:T(8,128)(2,1)S(1)} %pad_maximum_fusion.1.k0.v0), channel_id=1, source_target_pairs={{0,1},{1,2},{2,3},{3,4},{4,5},{5,6},{6,7},{8,9},{9,10},{10,11},{11... | collective-permute-start | bytes 7864328 | tf_op jit(solution)/shard_map/ppermute | solution.py:21
  33.4 286.7 %collective-permute-start.2 = (bf16[1024,1024]{1,0:T(8,128)(2,1)}, bf16[1024,1024]{1,0:T(8,128)(2,1)}, u32[]{:S(2)}, u32[]{:S(2)}) collective-permute-start(bf16[1024,1024]{1,0:T(8,128)(2,1)} %pad_maximum_fusion.3.k0.v0), channel_id=1, source_target_pairs={{0,1},{1,2},{2,3},{3,4},{4,5},{5,6},{6,7},{8,9},{9,10},{10,11},{11... | collective-permute-start | bytes 6291464 | tf_op jit(solution)/shard_map/ppermute | solution.py:21
  39.7 298.1 %collective-permute-start.1 = (bf16[1024,1024]{1,0:T(8,128)(2,1)}, bf16[1024,1024]{1,0:T(8,128)(2,1)}, u32[]{:S(2)}, u32[]{:S(2)}) collective-permute-start(bf16[1024,1024]{1,0:T(8,128)(2,1)} %pad_maximum_fusion.2.k0.v0), channel_id=1, source_target_pairs={{1,0},{2,1},{3,2},{4,3},{5,4},{6,5},{7,6},{9,8},{10,9},{11,10},{12... | collective-permute-start | bytes 6291464 | tf_op jit(solution)/shard_map/ppermute | solution.py:21
  93.7 290.1 %collective-permute-start = (bf16[1024,1024]{1,0:T(8,128)(2,1)}, bf16[1024,1024]{1,0:T(8,128)(2,1)}, u32[]{:S(2)}, u32[]{:S(2)}) collective-permute-start(bf16[1024,1024]{1,0:T(8,128)(2,1)} %pad_maximum_fusion.2.k0.v0), channel_id=1, source_target_pairs={{0,1},{1,2},{2,3},{3,4},{4,5},{5,6},{6,7},{8,9},{9,10},{10,11},{11... | collective-permute-start | bytes 6291464 | tf_op jit(solution)/shard_map/ppermute | solution.py:21
  417.8 2.7 copy-start.2
  425.7 4.4 copy-start.3
  477.2 74.6 %copy-start.4 = (s32[4,5]{1,0:T(4,128)S(1)}, s32[4,5]{1,0:T(4,128)}, u32[]{:S(2)}) copy-start(s32[4,5]{1,0:T(4,128)} %param.7) | copy-start | bytes 244
  477.2 152.8 %all-to-all-start = ((bf16[8,32,6656]{2,0,1:T(8,128)(2,1)}), bf16[8,32,6656]{2,0,1:T(8,128)(2,1)S(1)}, u32[]{:S(2)}, u32[]{:S(2)}) async-start(bf16[8,32,6656]{2,0,1:T(8,128)(2,1)} %copy.25), calls=%async_computation | async-start | bytes 6815744 | tf_op jit(solution)/shard_map/all_to_all | solution.py:179
Sparse Core Ops, SparseCore 0:
  15.9 398.2 all-reduce.1

commit v3 on v2

--- a/solution.py
+++ b/solution.py
@@ -47,7 +47,7 @@
         top_ref[...] = new_top
 
 
-def near_kernel(flags_ref, q_ref, k0, v0, k1, v1, k2, v2, acc_ref, top_ref, sum_ref):
+def near_kernel(flags_ref, q_ref, k0, v0, k1, v1, k2, v2, acc_prev, top_prev, sum_prev, acc_ref, top_ref, sum_ref):
     query = q_ref[...]
     numerator, largest, totals = block_terms(query, k0, v0)
     acc_ref[...] = numerator
@@ -65,39 +65,42 @@
     o_ref[...] = (acc_ref[...] / sum_ref[...]).astype(o_ref.dtype)
 
 
-def attend_near(flags, query_cols, blocks, head_count):
+def attend_near(flags, query_cols, blocks, first_head, head_count, state):
     q_spec = pl.BlockSpec((TOK, HD), lambda h, flags: (0, h))
     v_spec = pl.BlockSpec((TOK, HD), lambda h, flags: (0, head_count + h))
-    stat_spec = pl.BlockSpec((1, TOK, 1), lambda h, flags: (h, 0, 0))
+    acc_spec = pl.BlockSpec((TOK, HD), lambda h, flags: (0, first_head + h))
+    stat_spec = pl.BlockSpec((1, TOK, 1), lambda h, flags: (first_head + h, 0, 0))
+    held = pl.BlockSpec(memory_space=pl.ANY)
     operands = []
     for both in blocks:
         operands += [both, both]
+    count = 1 + len(operands)
     return pl.pallas_call(
         near_kernel,
         grid_spec=pltpu.PrefetchScalarGridSpec(
             num_scalar_prefetch=1,
             grid=(head_count,),
-            in_specs=[q_spec] + [q_spec, v_spec] * len(blocks),
-            out_specs=[q_spec, stat_spec, stat_spec],
+            in_specs=[q_spec] + [q_spec, v_spec] * len(blocks) + [held] * 3,
+            out_specs=[acc_spec, stat_spec, stat_spec],
         ),
         out_shape=[
-            jax.ShapeDtypeStruct((TOK, head_count * HD), jnp.float32),
-            jax.ShapeDtypeStruct((head_count, TOK, 1), jnp.float32),
-            jax.ShapeDtypeStruct((head_count, TOK, 1), jnp.float32),
+            jax.ShapeDtypeStruct((TOK, HH), jnp.float32),
+            jax.ShapeDtypeStruct((HEADS, TOK, 1), jnp.float32),
+            jax.ShapeDtypeStruct((HEADS, TOK, 1), jnp.float32),
         ],
-    )(flags, query_cols, *operands)
-
-
-def attend_thumb(flags, query_tile, thumb, acc, top, totals):
+        input_output_aliases={count + 1: 0, count + 2: 1, count + 3: 2},
+    )(flags, query_cols, *operands, *state)
+
+
+def attend_thumb(flags, query_tile, thumb_keys, thumb_values, acc, top, totals):
     q_spec = pl.BlockSpec((TOK, HD), lambda h, flags: (0, h))
-    v_spec = pl.BlockSpec((TOK, HD), lambda h, flags: (0, HEADS + h))
     stat_spec = pl.BlockSpec((1, TOK, 1), lambda h, flags: (h, 0, 0))
     return pl.pallas_call(
         thumb_kernel,
         grid_spec=pltpu.PrefetchScalarGridSpec(
             num_scalar_prefetch=1,
             grid=(HEADS,),
-            in_specs=[q_spec, q_spec, v_spec, q_spec, stat_spec, stat_spec],
+            in_specs=[q_spec, q_spec, q_spec, q_spec, stat_spec, stat_spec],
             out_specs=q_spec,
             scratch_shapes=[
                 pltpu.VMEM((TOK, HD), jnp.float32),
@@ -106,7 +109,7 @@
             ],
         ),
         out_shape=jax.ShapeDtypeStruct((TOK, HH), jnp.bfloat16),
-    )(flags, query_tile, thumb, thumb, acc, top, totals)
+    )(flags, query_tile, thumb_keys, thumb_values, acc, top, totals)
 
 
 def pixel_shuffle(attended):
@@ -155,22 +158,24 @@
     )
     per_peer = SHUF // device_count
 
-    mine = jnp.where(
-        slot_index == thumb_slot,
-        jnp.concatenate([key_tile, value_tile], axis=1),
-        jnp.zeros((TOK, 2 * HH), jnp.bfloat16),
-    )
-    thumb = lax.psum(mine, "tile")
-    states = []
+    mine = slot_index == thumb_slot
+    thumb_keys = lax.psum(jnp.where(mine, key_tile, jnp.zeros_like(key_tile)), "tile")
+    thumb_values = lax.psum(jnp.where(mine, value_tile, jnp.zeros_like(value_tile)), "tile")
+    state = (
+        jnp.zeros((TOK, HH), jnp.float32),
+        jnp.zeros((HEADS, TOK, 1), jnp.float32),
+        jnp.zeros((HEADS, TOK, 1), jnp.float32),
+    )
     for first_head, end_head in HEAD_CHUNKS:
         head_count = end_head - first_head
         cols = slice(first_head * HD, end_head * HD)
         own = jnp.concatenate([key_tile[:, cols], value_tile[:, cols]], axis=1)
         left = passed_along(own, "tile", 1)
         right = passed_along(own, "tile", -1)
-        states.append(attend_near(flags, query_tile[:, cols], (own, left, right), head_count))
-    acc, top, totals = (jnp.concatenate(parts, axis=axis) for parts, axis in zip(zip(*states), (1, 0, 0)))
-    attended = attend_thumb(flags, query_tile, thumb, acc, top, totals)
+        state = attend_near(
+            flags, query_tile[:, cols], (own, left, right), first_head, head_count, state
+        )
+    attended = attend_thumb(flags, query_tile, thumb_keys, thumb_values, *state)
     shuffled = pixel_shuffle(attended)
     arranged = jnp.roll(
         shuffled.reshape(per_peer, device_count, 4 * HH), row_start % device_count, axis=1

time: 648 us -> 638 us (0.985); the launches traced: 649 us -> 629 us
  waiting for transfers between devices: 329 us -> 371 us
  starting transfers between devices: 138 us -> 96.4 us
  local copies, waits for them, and re-layouts: 68.3 us -> 55.3 us
    ppermute x6, starting transfers between devices: 63.3 us -> 20.2 us  [passed_along(): lax.ppermute(value, axis, [(source, source + steps) for source in range(i...]
    ppermute x6, waiting for transfers between devices: 265 us -> 305 us  [passed_along(): lax.ppermute(value, axis, [(source, source + steps) for source in range(i...]
    pallas_call x6 -> x0, local copies, waits for them, and re-layouts: 12.4 us -> none  [attend_near(): pl.pallas_call(near_kernel, grid_spec=pltpu.PrefetchScalarGridSpec(num_sc...]
    concatenate x2 -> x0, local copies, waits for them, and re-layouts: 8.69 us -> none  [body(): jnp.concatenate(parts, axis=axis)]
    another operation x0 -> x2, local copies, waits for them, and re-layouts: none -> 6.89 us
  transfers between devices with their start and end apart: 8 -> 8, of which waited for: 4 -> 4; matrix products, arithmetic and copies ran while one was open for 9% -> 6% of each run, Pallas kernels for 7% -> 7%
where the time goes in v3:
time: 638 us; the launch traced here: 629 us
  waiting for transfers between devices  371 us (58%)
  starting transfers between devices  96.4 us (15%)
  Pallas kernels  59.8 us (9%)
  local copies, waits for them, and re-layouts  55.3 us (9%)
  other arithmetic  27.7 us (4%)
  between operations  18.7 us (3%)
    ppermute x6, waiting for transfers between devices, passed_along(): lax.ppermute(value, axis, [(source, source + steps) for source in range(i...  305 us
    all_to_all x1, starting transfers between devices, body(): lax.all_to_all(arranged, ('dp', 'tile'), split_axis=1, concat_axis=1, til...  76.2 us
    all_to_all x1, waiting for transfers between devices, body(): lax.all_to_all(arranged, ('dp', 'tile'), split_axis=1, concat_axis=1, til...  64.7 us
    pallas_call x3, Pallas kernels, attend_near(): pl.pallas_call(near_kernel, grid_spec=pltpu.PrefetchScalarGridSpec(num_sc...  42.8 us
    ppermute x6, starting transfers between devices, passed_along(): lax.ppermute(value, axis, [(source, source + steps) for source in range(i...  20.2 us
    pallas_call x1, Pallas kernels, attend_thumb(): pl.pallas_call(thumb_kernel, grid_spec=pltpu.PrefetchScalarGridSpec(num_s...  16.9 us
  transfers between devices with their start and end apart: 8, of which 4 were waited for; matrix products, arithmetic and copies ran while one was open for 6% of the time, Pallas kernels for 7%

profile of v3, /device:TPU:0, one launch (start us, length us, event | category | flops | bytes accessed | tf_op | source)
XLA Modules:
  0.0 628.6 jit_solution(15935173376159619827)
XLA Ops:
  8.7 4.2 broadcast_select_fusion
  18.6 6.2 collective-permute-start.4
  26.5 3.7 collective-permute-start
  34.5 6.5 %collective-permute-start.2 = (bf16[1024,1024]{1,0:T(8,128)(2,1)}, bf16[1024,1024]{1,0:T(8,128)(2,1)}, u32[]{:S(2)}, u32[]{:S(2)}) collective-permute-start(bf16[1024,1024]{1,0:T(8,128)(2,1)} %pad_maximum_fusion.1.k0.v0), channel_id=1, source_target_pairs={{0,1},{1,2},{2,3},{3,4},{4,5},{5,6},{6,7},{8,9},{9,10},{10,11},{11... | collective-permute-start | bytes 6291464 | tf_op jit(solution)/shard_map/ppermute | solution.py:21
  41.0 104.6 %collective-permute-done.4.k1.v1 = bf16[1024,1024]{1,0:T(8,128)(2,1)} collective-permute-done((bf16[1024,1024]{1,0:T(8,128)(2,1)}, bf16[1024,1024]{1,0:T(8,128)(2,1)}, u32[]{:S(2)}, u32[]{:S(2)}) %collective-permute-start.4) | collective-permute-done | bytes 2097184 | tf_op jit(solution)/shard_map/ppermute | solution.py:21
  156.6 3.1 fusion.9
  159.7 3.5 broadcast_10_top_prev_sum_prev.2.clone.top_prev
  163.2 3.4 broadcast_10_top_prev_sum_prev.2.clone2.sum_prev
  166.6 3.3 broadcast_in_dim.37.acc_prev
  169.9 13.2 %shard_map.46 = (f32[1024,1664]{1,0:T(8,128)}, f32[13,1024,1]{2,1,0:T(8,128)}, f32[13,1024,1]{2,1,0:T(8,128)}) custom-call(s32[3]{0:T(128)} %add_convert_fusion.flags_ref, bf16[1024,512]{1,0:T(8,128)(2,1)} %get-tuple-element.35.q_ref, bf16[1024,1024]{1,0:T(8,128)(2,1)} %pad_maximum_fusion.2.k0.v0, ...), custom_call_target="tpu_custom_call", output_to_operand_aliasing={{0}: (8, {}), {1}: (9, {}), {2}: (10, {})} | custom-call | tf_op jit(solution)/shard_map/pallas_call | solution.py:78
  183.1 200.2 %collective-permute-done.2.k1.v1 = bf16[1024,1024]{1,0:T(8,128)(2,1)} collective-permute-done((bf16[1024,1024]{1,0:T(8,128)(2,1)}, bf16[1024,1024]{1,0:T(8,128)(2,1)}, u32[]{:S(2)}, u32[]{:S(2)}) %collective-permute-start.2) | collective-permute-done | bytes 2097184 | tf_op jit(solution)/shard_map/ppermute | solution.py:21
  383.3 13.4 %shard_map.47 = (f32[1024,1664]{1,0:T(8,128)}, f32[13,1024,1]{2,1,0:T(8,128)}, f32[13,1024,1]{2,1,0:T(8,128)}) custom-call(s32[3]{0:T(128)} %add_convert_fusion.flags_ref, bf16[1024,512]{1,0:T(8,128)(2,1)} %get-tuple-element.36.q_ref, bf16[1024,1024]{1,0:T(8,128)(2,1)} %pad_maximum_fusion.1.k0.v0, ...), custom_call_target="tpu_custom_call", output_to_operand_aliasing={{0}: (8, {}), {1}: (9, {}), {2}: (10, {})} | custom-call | tf_op jit(solution)/shard_map/pallas_call | solution.py:78
  396.7 16.2 %shard_map.48 = (f32[1024,1664]{1,0:T(8,128)}, f32[13,1024,1]{2,1,0:T(8,128)}, f32[13,1024,1]{2,1,0:T(8,128)}) custom-call(s32[3]{0:T(128)} %add_convert_fusion.flags_ref, bf16[1024,640]{1,0:T(8,128)(2,1)} %slice.120.q_ref, bf16[1024,1280]{1,0:T(8,128)(2,1)} %copy-done, ...), custom_call_target="tpu_custom_call", output_to_operand_aliasing={{0}: (8, {}), {1}: (9, {}), {2}: (10, {})} | custom-call | tf_op jit(solution)/shard_map/pallas_call | solution.py:78
  414.1 16.9 %shard_map.49 = bf16[1024,1664]{1,0:T(8,128)(2,1)} custom-call(s32[3]{0:T(128)} %add_convert_fusion.flags_ref, bf16[1024,1664]{1,0:T(8,128)(2,1)} %bitcast.59, bf16[1024,1664]{1,0:T(8,128)(2,1)} %get-tuple-element.23.k3, bf16[1024,1664]{1,0:T(8,128)(2,1)} %get-tuple-element.24.v3, f32[1024,1664]{1,0:T(8,128)} %get-tuple-element.20.acc_in, ...), custom_call_target="tpu_custom_call" | custom-call | tf_op jit(solution)/shard_map/pallas_call | solution.py:98
  431.1 6.8 %reshape.201 = bf16[16,2,16,2,1664]{4,3,2,1,0:T(2,128)(2,1)S(1)} reshape(bf16[1024,1664]{1,0:T(8,128)(2,1)} %shard_map.49) | data formatting | bytes 6815744 | tf_op jit(solution)/shard_map/reshape | solution.py:119
  437.9 4.3 copy.26
  442.2 7.3 %reshape_reshape.3 = bf16[8,32,6656]{2,1,0:T(8,128)(2,1)S(1)} reshape(bf16[16,16,2,2,1664]{4,3,2,1,0:T(2,128)(2,1)} %bitcast.64) | data formatting | bytes 6815744 | tf_op jit(solution)/shard_map/reshape;reshape | solution.py:181
  451.9 3.6 copy.23
  455.5 76.2 %all-to-all-start = ((bf16[8,32,6656]{2,0,1:T(8,128)(2,1)}), bf16[8,32,6656]{2,0,1:T(8,128)(2,1)S(1)}, u32[]{:S(2)}, u32[]{:S(2)}) async-start(bf16[8,32,6656]{2,0,1:T(8,128)(2,1)} %copy.23), calls=%async_computation | async-start | bytes 6815744 | tf_op jit(solution)/shard_map/all_to_all | solution.py:184
  532.5 7.6 %and_or_fusion = (pred[32]{0:T(512)(128)(4,1)S(1)}, s32[32,1]{0,1:T(1,128)S(1)}, s32[32]{0:T(128)S(1)}, pred[32]{0:T(512)(128)(4,1)S(1)}) fusion(s32[]{:T(128)} %bitcast.8, s32[]{:T(128)} %bitcast.7, s32[]{:T(128)} %bitcast.6, s32[]{:T(128)} %bitcast.5, s32[]{:T(128)} %bitcast.3, s32[]{:T(128)} %bitcast.2, s32[]{:T(128)} %bitcast.1, s32[]{:T(128)} %bitcast, ...), kind=kLoop, calls=%fused_computation.29 | loop fusion | flops 1120 | bytes 368 | tf_op jit(solution)/shard_map/or | solution.py:191
  540.1 5.1 and_select_fusion
  545.3 64.7 %all-to-all-done = bf16[8,32,6656]{2,0,1:T(8,128)(2,1)S(1)} async-done(((bf16[8,32,6656]{2,0,1:T(8,128)(2,1)}), bf16[8,32,6656]{2,0,1:T(8,128)(2,1)S(1)}, u32[]{:S(2)}, u32[]{:S(2)}) %all-to-all-start) | async-done | bytes 3407904 | tf_op jit(solution)/shard_map/all_to_all | solution.py:184
  610.0 2.7 copy.24
  612.7 8.8 %scatter_custom_fusion = bf16[288,6656]{1,0:T(8,128)(2,1)} fusion(s32[256]{0:T(256)S(1)} %bitcast.66, bf16[256,6656]{1,0:T(8,128)(2,1)} %bitcast.65, bf16[]{:T(256)} %constant.99.clone.1), kind=kCustom, calls=%fused_computation.11 | custom fusion | bytes 3834368 | tf_op jit(solution)/shard_map/scatter | solution.py:202
  (37 shorter events, 24.3 us)
Async XLA Ops:
  6.5 407.6 %all-reduce.3.cloned.1.call-start = ((), (), s32[]{:S(2)}) async-start(), calls=%async_computation.1 | async-start | bytes 13631488 | tf_op jit(solution)/shard_map/psum | solution.py:162
  8.7 4.3 copy-start.1
  18.6 126.9 %collective-permute-start.4 = (bf16[1024,1024]{1,0:T(8,128)(2,1)}, bf16[1024,1024]{1,0:T(8,128)(2,1)}, u32[]{:S(2)}, u32[]{:S(2)}) collective-permute-start(bf16[1024,1024]{1,0:T(8,128)(2,1)} %pad_maximum_fusion.2.k0.v0), channel_id=1, source_target_pairs={{0,1},{1,2},{2,3},{3,4},{4,5},{5,6},{6,7},{8,9},{9,10},{10,11},{11... | collective-permute-start | bytes 6291464 | tf_op jit(solution)/shard_map/ppermute | solution.py:21
  26.5 129.5 %copy-start = (bf16[1024,1280]{1,0:T(8,128)(2,1)}, bf16[1024,1280]{1,0:T(8,128)(2,1)S(1)}, u32[]{:S(2)}) copy-start(bf16[1024,1280]{1,0:T(8,128)(2,1)S(1)} %pad_maximum_fusion.k0.v0) | copy-start | bytes 7864324
  26.5 370.2 %collective-permute-start = (bf16[1024,1280]{1,0:T(8,128)(2,1)S(1)}, bf16[1024,1280]{1,0:T(8,128)(2,1)}, u32[]{:S(2)}, u32[]{:S(2)}) collective-permute-start(bf16[1024,1280]{1,0:T(8,128)(2,1)S(1)} %pad_maximum_fusion.k0.v0), channel_id=1, source_target_pairs={{0,1},{1,2},{2,3},{3,4},{4,5},{5,6},{6,7},{8,9},{9,10},{10,11},{11... | collective-permute-start | bytes 7864328 | tf_op jit(solution)/shard_map/ppermute | solution.py:21
  30.2 366.5 %collective-permute-start.1 = (bf16[1024,1280]{1,0:T(8,128)(2,1)S(1)}, bf16[1024,1280]{1,0:T(8,128)(2,1)}, u32[]{:S(2)}, u32[]{:S(2)}) collective-permute-start(bf16[1024,1280]{1,0:T(8,128)(2,1)S(1)} %pad_maximum_fusion.k0.v0), channel_id=1, source_target_pairs={{1,0},{2,1},{3,2},{4,3},{5,4},{6,5},{7,6},{9,8},{10,9},{11,10},{12... | collective-permute-start | bytes 7864328 | tf_op jit(solution)/shard_map/ppermute | solution.py:21
  31.5 128.2 %collective-permute-start.5 = (bf16[1024,1024]{1,0:T(8,128)(2,1)}, bf16[1024,1024]{1,0:T(8,128)(2,1)}, u32[]{:S(2)}, u32[]{:S(2)}) collective-permute-start(bf16[1024,1024]{1,0:T(8,128)(2,1)} %pad_maximum_fusion.2.k0.v0), channel_id=1, source_target_pairs={{1,0},{2,1},{3,2},{4,3},{5,4},{6,5},{7,6},{9,8},{10,9},{11,10},{12... | collective-permute-start | bytes 6291464 | tf_op jit(solution)/shard_map/ppermute | solution.py:21
  34.5 348.8 %collective-permute-start.2 = (bf16[1024,1024]{1,0:T(8,128)(2,1)}, bf16[1024,1024]{1,0:T(8,128)(2,1)}, u32[]{:S(2)}, u32[]{:S(2)}) collective-permute-start(bf16[1024,1024]{1,0:T(8,128)(2,1)} %pad_maximum_fusion.1.k0.v0), channel_id=1, source_target_pairs={{0,1},{1,2},{2,3},{3,4},{4,5},{5,6},{6,7},{8,9},{9,10},{10,11},{11... | collective-permute-start | bytes 6291464 | tf_op jit(solution)/shard_map/ppermute | solution.py:21
  145.5 237.7 %collective-permute-start.3 = (bf16[1024,1024]{1,0:T(8,128)(2,1)}, bf16[1024,1024]{1,0:T(8,128)(2,1)}, u32[]{:S(2)}, u32[]{:S(2)}) collective-permute-start(bf16[1024,1024]{1,0:T(8,128)(2,1)} %pad_maximum_fusion.1.k0.v0), channel_id=1, source_target_pairs={{1,0},{2,1},{3,2},{4,3},{5,4},{6,5},{7,6},{9,8},{10,9},{11,10},{12... | collective-permute-start | bytes 6291464 | tf_op jit(solution)/shard_map/ppermute | solution.py:21
  455.5 76.2 %copy-start.2 = (s32[4,5]{1,0:T(4,128)S(1)}, s32[4,5]{1,0:T(4,128)}, u32[]{:S(2)}) copy-start(s32[4,5]{1,0:T(4,128)} %param.7) | copy-start | bytes 244
  455.5 154.4 %all-to-all-start = ((bf16[8,32,6656]{2,0,1:T(8,128)(2,1)}), bf16[8,32,6656]{2,0,1:T(8,128)(2,1)S(1)}, u32[]{:S(2)}, u32[]{:S(2)}) async-start(bf16[8,32,6656]{2,0,1:T(8,128)(2,1)} %copy.23), calls=%async_computation | async-start | bytes 6815744 | tf_op jit(solution)/shard_map/all_to_all | solution.py:184
Sparse Core Ops, SparseCore 0:
  15.1 399.0 all-reduce.2

commit v4 on v3

--- a/solution.py
+++ b/solution.py
@@ -157,6 +157,11 @@
         starts[page_index] + texts[page_index] + jnp.where(is_thumb, tile_total, grid_pos) * SHUF
     )
     per_peer = SHUF // device_count
+    query_tile = jnp.roll(
+        pixel_shuffle(query_tile).reshape(per_peer, device_count, 4 * HH),
+        row_start % device_count,
+        axis=1,
+    ).reshape(TOK, HH)
 
     mine = slot_index == thumb_slot
     thumb_keys = lax.psum(jnp.where(mine, key_tile, jnp.zeros_like(key_tile)), "tile")
@@ -176,10 +181,7 @@
             flags, query_tile[:, cols], (own, left, right), first_head, head_count, state
         )
     attended = attend_thumb(flags, query_tile, thumb_keys, thumb_values, *state)
-    shuffled = pixel_shuffle(attended)
-    arranged = jnp.roll(
-        shuffled.reshape(per_peer, device_count, 4 * HH), row_start % device_count, axis=1
-    )
+    arranged = attended.reshape(per_peer, device_count, 4 * HH)
     arranged = jnp.where(is_live, arranged, jnp.zeros_like(arranged))
     arrived = lax.all_to_all(arranged, ("dp", "tile"), split_axis=1, concat_axis=1, tiled=True)
     own_rank = page_index * slot_count + slot_index

time: 638 us -> 607 us (0.951); the launches traced: 629 us -> 613 us
  waiting for transfers between devices: 371 us -> 344 us
  local copies, waits for them, and re-layouts: 55.3 us -> 63.7 us
    ppermute x6, waiting for transfers between devices: 305 us -> 277 us  [passed_along(): lax.ppermute(value, axis, [(source, source + steps) for source in range(i...]
    another operation x3 -> x4, local copies, waits for them, and re-layouts: 14.2 us -> 20.8 us  [the longest x1 7.29 us: body(): pixel_shuffle(query_tile).reshape(per_peer, device_count, 4 * HH)]
  transfers between devices with their start and end apart: 8 -> 8, of which waited for: 4 -> 4; matrix products, arithmetic and copies ran while one was open for 6% -> 11% of each run, Pallas kernels for 7% -> 7%
where the time goes in v4:
time: 607 us; the launch traced here: 613 us
  waiting for transfers between devices  344 us (57%)
  starting transfers between devices  93.9 us (15%)
  local copies, waits for them, and re-layouts  63.7 us (10%)
  Pallas kernels  60.1 us (10%)
  other arithmetic  32.8 us (5%)
  between operations  19 us (3%)
    ppermute x6, waiting for transfers between devices, passed_along(): lax.ppermute(value, axis, [(source, source + steps) for source in range(i...  277 us
    all_to_all x1, starting transfers between devices, body(): lax.all_to_all(arranged, ('dp', 'tile'), split_axis=1, concat_axis=1, til...  73.5 us
    all_to_all x1, waiting for transfers between devices, body(): lax.all_to_all(arranged, ('dp', 'tile'), split_axis=1, concat_axis=1, til...  65 us
    pallas_call x3, Pallas kernels, attend_near(): pl.pallas_call(near_kernel, grid_spec=pltpu.PrefetchScalarGridSpec(num_sc...  43.1 us
    ppermute x6, starting transfers between devices, passed_along(): lax.ppermute(value, axis, [(source, source + steps) for source in range(i...  20.4 us
    pallas_call x1, Pallas kernels, attend_thumb(): pl.pallas_call(thumb_kernel, grid_spec=pltpu.PrefetchScalarGridSpec(num_s...  17 us
  transfers between devices with their start and end apart: 8, of which 4 were waited for; matrix products, arithmetic and copies ran while one was open for 11% of the time, Pallas kernels for 7%

profile of v4, /device:TPU:0, one launch (start us, length us, event | category | flops | bytes accessed | tf_op | source)
XLA Modules:
  0.0 613.0 jit_solution(3867568445092334998)
XLA Ops:
  8.7 4.1 broadcast_select_fusion
  18.6 6.2 %collective-permute-start.4 = (bf16[1024,1024]{1,0:T(8,128)(2,1)}, bf16[1024,1024]{1,0:T(8,128)(2,1)}, u32[]{:S(2)}, u32[]{:S(2)}) collective-permute-start(bf16[1024,1024]{1,0:T(8,128)(2,1)} %pad_maximum_fusion.2.k0.v0), channel_id=1, source_target_pairs={{0,1},{1,2},{2,3},{3,4},{4,5},{5,6},{6,7},{8,9},{9,10},{10,11},{11... | collective-permute-start | bytes 6291464 | tf_op jit(solution)/shard_map/ppermute | solution.py:21
  27.9 3.7 collective-permute-start
  35.9 6.5 %collective-permute-start.2 = (bf16[1024,1024]{1,0:T(8,128)(2,1)}, bf16[1024,1024]{1,0:T(8,128)(2,1)}, u32[]{:S(2)}, u32[]{:S(2)}) collective-permute-start(bf16[1024,1024]{1,0:T(8,128)(2,1)} %pad_maximum_fusion.1.k0.v0), channel_id=1, source_target_pairs={{0,1},{1,2},{2,3},{3,4},{4,5},{5,6},{6,7},{8,9},{9,10},{10,11},{11... | collective-permute-start | bytes 6291464 | tf_op jit(solution)/shard_map/ppermute | solution.py:21
  42.4 103.9 %collective-permute-done.4.k1.v1 = bf16[1024,1024]{1,0:T(8,128)(2,1)} collective-permute-done((bf16[1024,1024]{1,0:T(8,128)(2,1)}, bf16[1024,1024]{1,0:T(8,128)(2,1)}, u32[]{:S(2)}, u32[]{:S(2)}) %collective-permute-start.4) | collective-permute-done | bytes 2097184 | tf_op jit(solution)/shard_map/ppermute | solution.py:21
  154.2 6.6 %reshape_reshape.6 = bf16[16,2,16,2,1664]{4,3,2,1,0:T(2,128)(2,1)S(1)} reshape(bf16[1,1,1024,1664]{3,2,1,0:T(8,128)(2,1)} %param.4) | data formatting | bytes 6815744 | tf_op jit(solution)/shard_map/reshape;reshape | solution.py:119
  160.9 4.3 copy.21
  165.2 7.3 %reshape_reshape.7 = bf16[8,32,6656]{2,1,0:T(8,128)(2,1)S(1)} reshape(bf16[16,16,2,2,1664]{4,3,2,1,0:T(2,128)(2,1)} %copy.21) | data formatting | bytes 6815744 | tf_op jit(solution)/shard_map/reshape;reshape | solution.py:161
  172.5 4.0 fusion
  176.4 5.4 reshape.199.q_ref
  186.2 3.5 broadcast_10_top_prev_sum_prev.2.clone.top_prev
  189.7 3.4 broadcast_10_top_prev_sum_prev.2.clone2.sum_prev
  196.4 13.5 %shard_map.46 = (f32[1024,1664]{1,0:T(8,128)}, f32[13,1024,1]{2,1,0:T(8,128)}, f32[13,1024,1]{2,1,0:T(8,128)}) custom-call(s32[3]{0:T(128)} %add_convert_fusion.flags_ref, bf16[1024,512]{1,0:T(8,128)(2,1)} %get-tuple-element.35.q_ref, bf16[1024,1024]{1,0:T(8,128)(2,1)} %pad_maximum_fusion.2.k0.v0, ...), custom_call_target="tpu_custom_call", output_to_operand_aliasing={{0}: (8, {}), {1}: (9, {}), {2}: (10, {})} | custom-call | tf_op jit(solution)/shard_map/pallas_call | solution.py:78
  209.8 173.4 %collective-permute-done.2.k1.v1 = bf16[1024,1024]{1,0:T(8,128)(2,1)} collective-permute-done((bf16[1024,1024]{1,0:T(8,128)(2,1)}, bf16[1024,1024]{1,0:T(8,128)(2,1)}, u32[]{:S(2)}, u32[]{:S(2)}) %collective-permute-start.2) | collective-permute-done | bytes 2097184 | tf_op jit(solution)/shard_map/ppermute | solution.py:21
  383.3 13.7 %shard_map.47 = (f32[1024,1664]{1,0:T(8,128)}, f32[13,1024,1]{2,1,0:T(8,128)}, f32[13,1024,1]{2,1,0:T(8,128)}) custom-call(s32[3]{0:T(128)} %add_convert_fusion.flags_ref, bf16[1024,512]{1,0:T(8,128)(2,1)} %get-tuple-element.36.q_ref, bf16[1024,1024]{1,0:T(8,128)(2,1)} %pad_maximum_fusion.1.k0.v0, ...), custom_call_target="tpu_custom_call", output_to_operand_aliasing={{0}: (8, {}), {1}: (9, {}), {2}: (10, {})} | custom-call | tf_op jit(solution)/shard_map/pallas_call | solution.py:78
  397.0 16.0 %shard_map.48 = (f32[1024,1664]{1,0:T(8,128)}, f32[13,1024,1]{2,1,0:T(8,128)}, f32[13,1024,1]{2,1,0:T(8,128)}) custom-call(s32[3]{0:T(128)} %add_convert_fusion.flags_ref, bf16[1024,640]{1,0:T(8,128)(2,1)} %slice.120.q_ref, bf16[1024,1280]{1,0:T(8,128)(2,1)} %pad_maximum_fusion.k0.v0, ...), custom_call_target="tpu_custom_call", output_to_operand_aliasing={{0}: (8, {}), {1}: (9, {}), {2}: (10, {})} | custom-call | tf_op jit(solution)/shard_map/pallas_call | solution.py:78
  414.2 17.0 %shard_map.49 = bf16[1024,1664]{1,0:T(8,128)(2,1)} custom-call(s32[3]{0:T(128)} %add_convert_fusion.flags_ref, bf16[1024,1664]{1,0:T(8,128)(2,1)} %copy-done, bf16[1024,1664]{1,0:T(8,128)(2,1)} %get-tuple-element.23.k3, bf16[1024,1664]{1,0:T(8,128)(2,1)} %get-tuple-element.24.v3, f32[1024,1664]{1,0:T(8,128)} %get-tuple-element.20.acc_in, ...), custom_call_target="tpu_custom_call" | custom-call | tf_op jit(solution)/shard_map/pallas_call | solution.py:98
  433.4 3.7 select_n.187
  437.1 5.5 copy.24
  442.7 73.5 %all-to-all-start = ((bf16[8,32,6656]{2,0,1:T(8,128)(2,1)}), bf16[8,32,6656]{2,0,1:T(8,128)(2,1)S(1)}, u32[]{:S(2)}, u32[]{:S(2)}) async-start(bf16[8,32,6656]{2,0,1:T(8,128)(2,1)} %copy.24), calls=%async_computation | async-start | bytes 6815744 | tf_op jit(solution)/shard_map/all_to_all | solution.py:186
  516.8 7.4 %and_or_fusion = (pred[32]{0:T(512)(128)(4,1)S(1)}, s32[32,1]{0,1:T(1,128)S(1)}, s32[32]{0:T(128)S(1)}, pred[32]{0:T(512)(128)(4,1)S(1)}) fusion(s32[]{:T(128)} %bitcast.8, s32[]{:T(128)} %bitcast.7, s32[]{:T(128)} %bitcast.6, s32[]{:T(128)} %bitcast.5, s32[]{:T(128)} %bitcast.3, s32[]{:T(128)} %bitcast.2, s32[]{:T(128)} %bitcast.1, s32[]{:T(128)} %bitcast, ...), kind=kLoop, calls=%fused_computation.28 | loop fusion | flops 1120 | bytes 368 | tf_op jit(solution)/shard_map/or | solution.py:193
  524.2 5.1 and_select_fusion
  529.4 65.0 %all-to-all-done = bf16[8,32,6656]{2,0,1:T(8,128)(2,1)S(1)} async-done(((bf16[8,32,6656]{2,0,1:T(8,128)(2,1)}), bf16[8,32,6656]{2,0,1:T(8,128)(2,1)S(1)}, u32[]{:S(2)}, u32[]{:S(2)}) %all-to-all-start) | async-done | bytes 3407904 | tf_op jit(solution)/shard_map/all_to_all | solution.py:186
  597.1 8.8 %scatter_custom_fusion = bf16[288,6656]{1,0:T(8,128)(2,1)} fusion(s32[256]{0:T(256)S(1)} %bitcast.62, bf16[256,6656]{1,0:T(8,128)(2,1)} %bitcast.61, bf16[]{:T(256)} %constant.99.clone.1), kind=kCustom, calls=%fused_computation.10 | custom fusion | bytes 3834368 | tf_op jit(solution)/shard_map/scatter | solution.py:204
  (40 shorter events, 32.6 us)
Async XLA Ops:
  6.5 407.6 %all-reduce.3.cloned.1.call-start = ((), (), s32[]{:S(2)}) async-start(), calls=%async_computation.1 | async-start | bytes 13631488 | tf_op jit(solution)/shard_map/psum | solution.py:167
  8.7 4.1 copy-start.1
  18.6 127.7 %collective-permute-start.4 = (bf16[1024,1024]{1,0:T(8,128)(2,1)}, bf16[1024,1024]{1,0:T(8,128)(2,1)}, u32[]{:S(2)}, u32[]{:S(2)}) collective-permute-start(bf16[1024,1024]{1,0:T(8,128)(2,1)} %pad_maximum_fusion.2.k0.v0), channel_id=1, source_target_pairs={{0,1},{1,2},{2,3},{3,4},{4,5},{5,6},{6,7},{8,9},{9,10},{10,11},{11... | collective-permute-start | bytes 6291464 | tf_op jit(solution)/shard_map/ppermute | solution.py:21
  27.9 369.0 %collective-permute-start = (bf16[1024,1280]{1,0:T(8,128)(2,1)}, bf16[1024,1280]{1,0:T(8,128)(2,1)}, u32[]{:S(2)}, u32[]{:S(2)}) collective-permute-start(bf16[1024,1280]{1,0:T(8,128)(2,1)} %pad_maximum_fusion.k0.v0), channel_id=1, source_target_pairs={{0,1},{1,2},{2,3},{3,4},{4,5},{5,6},{6,7},{8,9},{9,10},{10,11},{11... | collective-permute-start | bytes 7864328 | tf_op jit(solution)/shard_map/ppermute | solution.py:21
  31.6 365.3 %collective-permute-start.1 = (bf16[1024,1280]{1,0:T(8,128)(2,1)}, bf16[1024,1280]{1,0:T(8,128)(2,1)}, u32[]{:S(2)}, u32[]{:S(2)}) collective-permute-start(bf16[1024,1280]{1,0:T(8,128)(2,1)} %pad_maximum_fusion.k0.v0), channel_id=1, source_target_pairs={{1,0},{2,1},{3,2},{4,3},{5,4},{6,5},{7,6},{9,8},{10,9},{11,10},{12... | collective-permute-start | bytes 7864328 | tf_op jit(solution)/shard_map/ppermute | solution.py:21
  32.9 153.3 %collective-permute-start.5 = (bf16[1024,1024]{1,0:T(8,128)(2,1)}, bf16[1024,1024]{1,0:T(8,128)(2,1)}, u32[]{:S(2)}, u32[]{:S(2)}) collective-permute-start(bf16[1024,1024]{1,0:T(8,128)(2,1)} %pad_maximum_fusion.2.k0.v0), channel_id=1, source_target_pairs={{1,0},{2,1},{3,2},{4,3},{5,4},{6,5},{7,6},{9,8},{10,9},{11,10},{12... | collective-permute-start | bytes 6291464 | tf_op jit(solution)/shard_map/ppermute | solution.py:21
  35.9 347.3 %collective-permute-start.2 = (bf16[1024,1024]{1,0:T(8,128)(2,1)}, bf16[1024,1024]{1,0:T(8,128)(2,1)}, u32[]{:S(2)}, u32[]{:S(2)}) collective-permute-start(bf16[1024,1024]{1,0:T(8,128)(2,1)} %pad_maximum_fusion.1.k0.v0), channel_id=1, source_target_pairs={{0,1},{1,2},{2,3},{3,4},{4,5},{5,6},{6,7},{8,9},{9,10},{10,11},{11... | collective-permute-start | bytes 6291464 | tf_op jit(solution)/shard_map/ppermute | solution.py:21
  146.3 237.0 %collective-permute-start.3 = (bf16[1024,1024]{1,0:T(8,128)(2,1)}, bf16[1024,1024]{1,0:T(8,128)(2,1)}, u32[]{:S(2)}, u32[]{:S(2)}) collective-permute-start(bf16[1024,1024]{1,0:T(8,128)(2,1)} %pad_maximum_fusion.1.k0.v0), channel_id=1, source_target_pairs={{1,0},{2,1},{3,2},{4,3},{5,4},{6,5},{7,6},{9,8},{10,9},{11,10},{12... | collective-permute-start | bytes 6291464 | tf_op jit(solution)/shard_map/ppermute | solution.py:21
  181.9 4.3 copy-start
  442.7 73.5 %copy-start.2 = (s32[4,5]{1,0:T(4,128)S(1)}, s32[4,5]{1,0:T(4,128)}, u32[]{:S(2)}) copy-start(s32[4,5]{1,0:T(4,128)} %param.7) | copy-start | bytes 244
  442.7 151.8 %all-to-all-start = ((bf16[8,32,6656]{2,0,1:T(8,128)(2,1)}), bf16[8,32,6656]{2,0,1:T(8,128)(2,1)S(1)}, u32[]{:S(2)}, u32[]{:S(2)}) async-start(bf16[8,32,6656]{2,0,1:T(8,128)(2,1)} %copy.24), calls=%async_computation | async-start | bytes 6815744 | tf_op jit(solution)/shard_map/all_to_all | solution.py:186
Sparse Core Ops, SparseCore 0:
  15.1 399.0 all-reduce.2

commit v5 on v4

--- a/solution.py
+++ b/solution.py
@@ -171,12 +171,18 @@
         jnp.zeros((HEADS, TOK, 1), jnp.float32),
         jnp.zeros((HEADS, TOK, 1), jnp.float32),
     )
+    arrived_last = None
+    state_before = None
     for first_head, end_head in HEAD_CHUNKS:
         head_count = end_head - first_head
         cols = slice(first_head * HD, end_head * HD)
         own = jnp.concatenate([key_tile[:, cols], value_tile[:, cols]], axis=1)
+        if arrived_last is not None:
+            arrived_last, state_before, own = lax.optimization_barrier((arrived_last, state_before, own))
         left = passed_along(own, "tile", 1)
         right = passed_along(own, "tile", -1)
+        arrived_last = (left, right)
+        state_before = state
         state = attend_near(
             flags, query_tile[:, cols], (own, left, right), first_head, head_count, state
         )

time: 607 us -> 592 us (0.975); the launches traced: 613 us -> 582 us
  waiting for transfers between devices: 344 us -> 324 us
  starting transfers between devices: 93.9 us -> 77.1 us
    ppermute x6, waiting for transfers between devices: 277 us -> 259 us  [passed_along(): lax.ppermute(value, axis, [(source, source + steps) for source in range(i...]
    all_to_all x1, starting transfers between devices: 73.5 us -> 55.5 us  [body(): lax.all_to_all(arranged, ('dp', 'tile'), split_axis=1, concat_axis=1, til...]
  transfers between devices with their start and end apart: 8 -> 8, of which waited for: 4 -> 4; matrix products, arithmetic and copies ran while one was open for 11% -> 13% of each run, Pallas kernels for 7% -> 7%
where the time goes in v5:
time: 592 us; the launch traced here: 582 us
  waiting for transfers between devices  324 us (55%)
  starting transfers between devices  77.1 us (13%)
  local copies, waits for them, and re-layouts  69.2 us (12%)
  Pallas kernels  60 us (10%)
  other arithmetic  31.7 us (5%)
  between operations  19.2 us (3%)
    ppermute x6, waiting for transfers between devices, passed_along(): lax.ppermute(value, axis, [(source, source + steps) for source in range(i...  259 us
    all_to_all x1, waiting for transfers between devices, body(): lax.all_to_all(arranged, ('dp', 'tile'), split_axis=1, concat_axis=1, til...  65 us
    all_to_all x1, starting transfers between devices, body(): lax.all_to_all(arranged, ('dp', 'tile'), split_axis=1, concat_axis=1, til...  55.5 us
    pallas_call x3, Pallas kernels, attend_near(): pl.pallas_call(near_kernel, grid_spec=pltpu.PrefetchScalarGridSpec(num_sc...  43 us
    ppermute x6, starting transfers between devices, passed_along(): lax.ppermute(value, axis, [(source, source + steps) for source in range(i...  21.7 us
    pallas_call x1, Pallas kernels, attend_thumb(): pl.pallas_call(thumb_kernel, grid_spec=pltpu.PrefetchScalarGridSpec(num_s...  17 us
  transfers between devices with their start and end apart: 8, of which 4 were waited for; matrix products, arithmetic and copies ran while one was open for 13% of the time, Pallas kernels for 7%

profile of v5, /device:TPU:0, one launch (start us, length us, event | category | flops | bytes accessed | tf_op | source)
XLA Modules:
  0.0 581.5 jit_solution(18433278534592729570)
XLA Ops:
  10.3 6.2 %collective-permute-start = (bf16[1024,1024]{1,0:T(8,128)(2,1)S(1)}, bf16[1024,1024]{1,0:T(8,128)(2,1)}, u32[]{:S(2)}, u32[]{:S(2)}) collective-permute-start(bf16[1024,1024]{1,0:T(8,128)(2,1)S(1)} %pad_maximum_fusion.1.k0.v0), channel_id=1, source_target_pairs={{0,1},{1,2},{2,3},{3,4},{4,5},{5,6},{6,7},{8,9},{9,10},{10,11},{11... | collective-permute-start | bytes 6291464 | tf_op jit(solution)/shard_map/ppermute | solution.py:21
  19.1 4.1 broadcast_select_fusion
  28.3 101.0 %collective-permute-done.k1.v1 = bf16[1024,1024]{1,0:T(8,128)(2,1)} collective-permute-done((bf16[1024,1024]{1,0:T(8,128)(2,1)S(1)}, bf16[1024,1024]{1,0:T(8,128)(2,1)}, u32[]{:S(2)}, u32[]{:S(2)}) %collective-permute-start) | collective-permute-done | bytes 2097184 | tf_op jit(solution)/shard_map/ppermute | solution.py:21
  129.3 5.8 collective-permute-start.2
  148.0 6.6 %reshape_reshape.6 = bf16[16,2,16,2,1664]{4,3,2,1,0:T(2,128)(2,1)S(1)} reshape(bf16[1,1,1024,1664]{3,2,1,0:T(8,128)(2,1)} %param.4) | data formatting | bytes 6815744 | tf_op jit(solution)/shard_map/reshape;reshape | solution.py:119
  154.6 4.3 copy.18
  158.9 7.3 %reshape_reshape.7 = bf16[8,32,6656]{2,1,0:T(8,128)(2,1)S(1)} reshape(bf16[16,16,2,2,1664]{4,3,2,1,0:T(2,128)(2,1)} %copy.18) | data formatting | bytes 6815744 | tf_op jit(solution)/shard_map/reshape;reshape | solution.py:161
  166.2 4.0 fusion
  170.2 5.4 reshape.199.q_ref
  180.9 3.5 broadcast_10_top_prev_sum_prev.2.clone.top_prev
  191.1 13.5 %shard_map.46 = (f32[1024,1664]{1,0:T(8,128)}, f32[13,1024,1]{2,1,0:T(8,128)}, f32[13,1024,1]{2,1,0:T(8,128)}) custom-call(s32[3]{0:T(128)} %add_convert_fusion.flags_ref, bf16[1024,512]{1,0:T(8,128)(2,1)} %get-tuple-element.36.q_ref, bf16[1024,1024]{1,0:T(8,128)(2,1)} %copy-done.1, ...), custom_call_target="tpu_custom_call", output_to_operand_aliasing={{0}: (8, {}), {1}: (9, {}), {2}: (10, {})} | custom-call | tf_op jit(solution)/shard_map/pallas_call | solution.py:78
  204.5 35.5 %collective-permute-done.2.k1.v1 = bf16[1024,1024]{1,0:T(8,128)(2,1)} collective-permute-done((bf16[1024,1024]{1,0:T(8,128)(2,1)}, bf16[1024,1024]{1,0:T(8,128)(2,1)}, u32[]{:S(2)}, u32[]{:S(2)}) %collective-permute-start.2) | collective-permute-done | bytes 2097184 | tf_op jit(solution)/shard_map/ppermute | solution.py:21
  240.1 5.9 %collective-permute-start.4 = (bf16[1024,1280]{1,0:T(8,128)(2,1)}, bf16[1024,1280]{1,0:T(8,128)(2,1)}, u32[]{:S(2)}, u32[]{:S(2)}) collective-permute-start(bf16[1024,1280]{1,0:T(8,128)(2,1)} %pad_maximum_fusion.k0.v0), channel_id=1, source_target_pairs={{0,1},{1,2},{2,3},{3,4},{4,5},{5,6},{6,7},{8,9},{9,10},{10,11},{11... | collective-permute-start | bytes 7864328 | tf_op jit(solution)/shard_map/ppermute | solution.py:21
  248.4 13.6 %shard_map.47 = (f32[1024,1664]{1,0:T(8,128)}, f32[13,1024,1]{2,1,0:T(8,128)}, f32[13,1024,1]{2,1,0:T(8,128)}) custom-call(s32[3]{0:T(128)} %add_convert_fusion.flags_ref, bf16[1024,512]{1,0:T(8,128)(2,1)} %get-tuple-element.35.q_ref, bf16[1024,1024]{1,0:T(8,128)(2,1)} %pad_maximum_fusion.2.k0.v0, ...), custom_call_target="tpu_custom_call", output_to_operand_aliasing={{0}: (8, {}), {1}: (9, {}), {2}: (10, {})} | custom-call | tf_op jit(solution)/shard_map/pallas_call | solution.py:78
  262.0 122.7 %collective-permute-done.4.k1.v1 = bf16[1024,1280]{1,0:T(8,128)(2,1)} collective-permute-done((bf16[1024,1280]{1,0:T(8,128)(2,1)}, bf16[1024,1280]{1,0:T(8,128)(2,1)}, u32[]{:S(2)}, u32[]{:S(2)}) %collective-permute-start.4) | collective-permute-done | bytes 2621472 | tf_op jit(solution)/shard_map/ppermute | solution.py:21
  384.7 15.9 %shard_map.48 = (f32[1024,1664]{1,0:T(8,128)}, f32[13,1024,1]{2,1,0:T(8,128)}, f32[13,1024,1]{2,1,0:T(8,128)}) custom-call(s32[3]{0:T(128)} %add_convert_fusion.flags_ref, bf16[1024,640]{1,0:T(8,128)(2,1)} %slice.120.q_ref, bf16[1024,1280]{1,0:T(8,128)(2,1)} %pad_maximum_fusion.k0.v0, ...), custom_call_target="tpu_custom_call", output_to_operand_aliasing={{0}: (8, {}), {1}: (9, {}), {2}: (10, {})} | custom-call | tf_op jit(solution)/shard_map/pallas_call | solution.py:78
  400.7 17.0 %shard_map.49 = bf16[1024,1664]{1,0:T(8,128)(2,1)} custom-call(s32[3]{0:T(128)} %add_convert_fusion.flags_ref, bf16[1024,1664]{1,0:T(8,128)(2,1)} %copy-done, bf16[1024,1664]{1,0:T(8,128)(2,1)} %get-tuple-element.27.k3, bf16[1024,1664]{1,0:T(8,128)(2,1)} %get-tuple-element.28.v3, f32[1024,1664]{1,0:T(8,128)} %get-tuple-element.24.acc_in, ...), custom_call_target="tpu_custom_call" | custom-call | tf_op jit(solution)/shard_map/pallas_call | solution.py:98
  419.9 3.7 select_n.187
  423.7 5.5 copy.19
  429.2 55.5 %all-to-all-start = ((bf16[8,32,6656]{2,0,1:T(8,128)(2,1)}), bf16[8,32,6656]{2,0,1:T(8,128)(2,1)S(1)}, u32[]{:S(2)}, u32[]{:S(2)}) async-start(bf16[8,32,6656]{2,0,1:T(8,128)(2,1)} %copy.19), calls=%async_computation | async-start | bytes 6815744 | tf_op jit(solution)/shard_map/all_to_all | solution.py:192
  485.4 7.5 %and_or_fusion = (pred[32]{0:T(512)(128)(4,1)S(1)}, s32[32,1]{0,1:T(1,128)S(1)}, s32[32]{0:T(128)S(1)}, pred[32]{0:T(512)(128)(4,1)S(1)}) fusion(s32[]{:T(128)} %bitcast.8, s32[]{:T(128)} %bitcast.7, s32[]{:T(128)} %bitcast.6, s32[]{:T(128)} %bitcast.5, s32[]{:T(128)} %bitcast.3, s32[]{:T(128)} %bitcast.2, s32[]{:T(128)} %bitcast.1, s32[]{:T(128)} %bitcast, ...), kind=kLoop, calls=%fused_computation.28 | loop fusion | flops 1120 | bytes 368 | tf_op jit(solution)/shard_map/or | solution.py:199
  492.9 5.0 and_select_fusion
  498.0 65.0 %all-to-all-done = bf16[8,32,6656]{2,0,1:T(8,128)(2,1)S(1)} async-done(((bf16[8,32,6656]{2,0,1:T(8,128)(2,1)}), bf16[8,32,6656]{2,0,1:T(8,128)(2,1)S(1)}, u32[]{:S(2)}, u32[]{:S(2)}) %all-to-all-start) | async-done | bytes 3407904 | tf_op jit(solution)/shard_map/all_to_all | solution.py:192
  565.7 8.8 %scatter_custom_fusion = bf16[288,6656]{1,0:T(8,128)(2,1)} fusion(s32[256]{0:T(256)S(1)} %bitcast.62, bf16[256,6656]{1,0:T(8,128)(2,1)} %bitcast.61, bf16[]{:T(256)} %constant.99.clone.1), kind=kCustom, calls=%fused_computation.10 | custom fusion | bytes 3834368 | tf_op jit(solution)/shard_map/scatter | solution.py:210
  (46 shorter events, 39.0 us)
Async XLA Ops:
  6.5 394.1 %all-reduce.3.cloned.1.call-start = ((), (), s32[]{:S(2)}) async-start(), calls=%async_computation.1 | async-start | bytes 13631488 | tf_op jit(solution)/shard_map/psum | solution.py:167
  10.0 7.8 %copy-start.5 = (s32[4,5]{1,0:T(4,128)S(1)}, s32[4,5]{1,0:T(4,128)}, u32[]{:S(2)}) copy-start(s32[4,5]{1,0:T(4,128)} %param.7) | copy-start | bytes 244
  10.3 13.0 %copy-start.1 = (bf16[1024,1024]{1,0:T(8,128)(2,1)}, bf16[1024,1024]{1,0:T(8,128)(2,1)S(1)}, u32[]{:S(2)}) copy-start(bf16[1024,1024]{1,0:T(8,128)(2,1)S(1)} %pad_maximum_fusion.1.k0.v0) | copy-start | bytes 6291460
  10.3 119.0 %collective-permute-start = (bf16[1024,1024]{1,0:T(8,128)(2,1)S(1)}, bf16[1024,1024]{1,0:T(8,128)(2,1)}, u32[]{:S(2)}, u32[]{:S(2)}) collective-permute-start(bf16[1024,1024]{1,0:T(8,128)(2,1)S(1)} %pad_maximum_fusion.1.k0.v0), channel_id=1, source_target_pairs={{0,1},{1,2},{2,3},{3,4},{4,5},{5,6},{6,7},{8,9},{9,10},{10,11},{11... | collective-permute-start | bytes 6291464 | tf_op jit(solution)/shard_map/ppermute | solution.py:21
  16.5 112.8 %collective-permute-start.1 = (bf16[1024,1024]{1,0:T(8,128)(2,1)S(1)}, bf16[1024,1024]{1,0:T(8,128)(2,1)}, u32[]{:S(2)}, u32[]{:S(2)}) collective-permute-start(bf16[1024,1024]{1,0:T(8,128)(2,1)S(1)} %pad_maximum_fusion.1.k0.v0), channel_id=1, source_target_pairs={{1,0},{2,1},{3,2},{4,3},{5,4},{6,5},{7,6},{9,8},{10,9},{11,10},{12... | collective-permute-start | bytes 6291464 | tf_op jit(solution)/shard_map/ppermute | solution.py:21
  19.1 4.1 copy-start.2
  129.3 110.8 %collective-permute-start.2 = (bf16[1024,1024]{1,0:T(8,128)(2,1)}, bf16[1024,1024]{1,0:T(8,128)(2,1)}, u32[]{:S(2)}, u32[]{:S(2)}) collective-permute-start(bf16[1024,1024]{1,0:T(8,128)(2,1)} %pad_maximum_fusion.2.k0.v0), channel_id=1, source_target_pairs={{0,1},{1,2},{2,3},{3,4},{4,5},{5,6},{6,7},{8,9},{9,10},{10,11},{11... | collective-permute-start | bytes 6291464 | tf_op jit(solution)/shard_map/ppermute | solution.py:21
  135.1 105.0 %collective-permute-start.3 = (bf16[1024,1024]{1,0:T(8,128)(2,1)}, bf16[1024,1024]{1,0:T(8,128)(2,1)}, u32[]{:S(2)}, u32[]{:S(2)}) collective-permute-start(bf16[1024,1024]{1,0:T(8,128)(2,1)} %pad_maximum_fusion.2.k0.v0), channel_id=1, source_target_pairs={{1,0},{2,1},{3,2},{4,3},{5,4},{6,5},{7,6},{9,8},{10,9},{11,10},{12... | collective-permute-start | bytes 6291464 | tf_op jit(solution)/shard_map/ppermute | solution.py:21
  175.6 71.7 %copy-start = (bf16[1024,1664]{1,0:T(8,128)(2,1)}, bf16[1024,1664]{1,0:T(8,128)(2,1)S(1)}, u32[]{:S(2)}) copy-start(bf16[1024,1664]{1,0:T(8,128)(2,1)S(1)} %reshape.199.q_ref) | copy-start | bytes 10223620
  176.3 2.2 copy-start.3
  176.3 2.9 copy-start.4
  240.1 144.6 %collective-permute-start.4 = (bf16[1024,1280]{1,0:T(8,128)(2,1)}, bf16[1024,1280]{1,0:T(8,128)(2,1)}, u32[]{:S(2)}, u32[]{:S(2)}) collective-permute-start(bf16[1024,1280]{1,0:T(8,128)(2,1)} %pad_maximum_fusion.k0.v0), channel_id=1, source_target_pairs={{0,1},{1,2},{2,3},{3,4},{4,5},{5,6},{6,7},{8,9},{9,10},{10,11},{11... | collective-permute-start | bytes 7864328 | tf_op jit(solution)/shard_map/ppermute | solution.py:21
  245.9 138.7 %collective-permute-start.5 = (bf16[1024,1280]{1,0:T(8,128)(2,1)}, bf16[1024,1280]{1,0:T(8,128)(2,1)}, u32[]{:S(2)}, u32[]{:S(2)}) collective-permute-start(bf16[1024,1280]{1,0:T(8,128)(2,1)} %pad_maximum_fusion.k0.v0), channel_id=1, source_target_pairs={{1,0},{2,1},{3,2},{4,3},{5,4},{6,5},{7,6},{9,8},{10,9},{11,10},{12... | collective-permute-start | bytes 7864328 | tf_op jit(solution)/shard_map/ppermute | solution.py:21
  429.2 133.8 %all-to-all-start = ((bf16[8,32,6656]{2,0,1:T(8,128)(2,1)}), bf16[8,32,6656]{2,0,1:T(8,128)(2,1)S(1)}, u32[]{:S(2)}, u32[]{:S(2)}) async-start(bf16[8,32,6656]{2,0,1:T(8,128)(2,1)} %copy.19), calls=%async_computation | async-start | bytes 6815744 | tf_op jit(solution)/shard_map/all_to_all | solution.py:192
Sparse Core Ops, SparseCore 0:
  25.5 370.2 all-reduce.2
